TPU v7x, 256 devices: a whole 4x4x8 slice. The times are simulated.
256 devices in a mesh: req: 16 (over x, z_hi, core), tp: 16 (over y, z_lo).
Axes of the slice: x: 4, y: 4, z: 8 (z_hi: 2, z_lo: 4; z = z_hi * 4 + z_lo), core: 2. Of those that a mesh axis runs over, the one named last changes fastest.
Arguments:
- tokens: bfloat16 [16, 512, 3200], P('req', 'tp'), may hold values from -6 to 6
- segments: int32 [16, 512], P('req'), may hold values from -1 to 7, as said below
- norm_gain: float32 [3200], replicated, may hold values from 0.25 to 1.75
- wqkv: bfloat16 [3, 3200, 2048], P(None, None, 'tp'), may hold values from -4 to 4
- qk_gain: float32 [2, 2048], P(None, 'tp'), may hold values from 0.6 to 4
- wproj: bfloat16 [2048, 3200], P('tp'), may hold values from -0.125 to 0.125
- bproj: float32 [3200], P('tp'), may hold values from -3 to 3
- layer_scale: float32 [3200], P('tp'), may hold values from 0.3 to 1.5
- ln_weight: float32 [4, 3200], P(None, 'tp'), may hold values from 0.25 to 1.75
- ln_bias: float32 [4, 3200], P(None, 'tp'), may hold values from -2 to 2
- w_merge: bfloat16 [4, 3200, 3072], P(None, 'tp'), may hold values from -0.0546875 to 0.0546875
- b_merge: float32 [3072], replicated, may hold values from -3 to 3
- owners: int32 [16, 128, 1], P(None, 'tp'), may hold values from 0 to 15; in each aligned block of 8 rows (0 to 7, 8 to 15, ..., all dimensions but the last counted through in order) at most 2 rows name the same one
Outputs:
- lm_inputs: bfloat16 [16, 16, 16, 2, 3072], P('req', None, 'tp')
Inputs may be any that keep to these rules, and one draw needn't show every extreme that they name: `segments`: each group's tokens are whole images, each a whole number of blocks of 64 tokens (two patch rows); image numbers start at 0 and never fall; padding tokens (-1) fill the end of a group from a block boundary; some group has no padding and some group has padding. `owners`: among the 8 merged tokens of one device (aligned blocks of one group), at most 2 name the same owner.
All inputs are finite; a program needn't handle non-finite values.
Results may differ from a plain program's by a relative error of at most 0.014.
Values may be sent and summed in bfloat16 or wider, within the bound.
No kernel may reach another device: no remote copies, remote signals or barrier semaphores. Data moves between devices by JAX's collectives and lax.ppermute only.
A program may use at most 64 MiB of HBM per device.

v0:
```python
import jax
import jax.numpy as jnp
from jax import lax
from jax.sharding import PartitionSpec as P

D = 3200
HEADS = 16
HD = 128
PW = 32


EPS_RMS = 1e-06
EPS_LN = 1e-05


def block_count(length):
    number = max(1, length // 512)
    while length % number:
        number = number - 1
    return number


def attend_block(query_rows, key_heads, value_heads, query_segs, key_segs):
    scores = jnp.einsum(
        "hqd,hkd->hqk", query_rows, key_heads, preferred_element_type=jnp.float32
    ) * HD ** (-0.5)
    same_image = query_segs[:, None] == key_segs[None, :]
    scores = jnp.where(same_image[None], scores, -jnp.inf)
    row_max = jnp.max(scores, axis=-1, keepdims=True)
    weights = jnp.exp(scores - row_max)
    probabilities = (weights / jnp.sum(weights, axis=-1, keepdims=True)).astype(jnp.bfloat16)
    mixed = jnp.einsum(
        "hqk,hkd->hqd", probabilities, value_heads, preferred_element_type=jnp.float32
    )
    return mixed.astype(jnp.bfloat16)


def merge_rows(stream):
    feature_count = stream.shape[-1]
    shaped = stream.reshape(stream.shape[0] // (2 * PW), 2, PW // 2, 2, feature_count)
    return shaped.transpose(0, 2, 1, 3, 4).reshape(stream.shape[0] // 4, 4, feature_count)


def slot_ranks(owner_ids, group_total):
    owner_hits = (owner_ids[:, None] == jnp.arange(group_total, dtype=jnp.int32)[None, :]).astype(
        jnp.int32
    )
    before = jnp.cumsum(owner_hits, axis=0) - owner_hits
    return jnp.sum(before * owner_hits, axis=1)


def per_device(
    tokens,
    segments,
    norm_gain,
    wqkv,
    qk_gain,
    wproj,
    bproj,
    layer_scale,
    ln_weight,
    ln_bias,
    w_merge,
    b_merge,
    owners,
):
    tp_total = lax.axis_size("tp")
    tp_index = lax.axis_index("tp")
    req_index = lax.axis_index("req")
    group_total = lax.axis_size("req")
    gathered = lax.all_gather(tokens, "tp", axis=1, tiled=True)[0]
    seq_len = gathered.shape[0]
    group_segs = segments[0]
    widened = gathered.astype(jnp.float32)
    normed = (
        widened
        * lax.rsqrt(jnp.mean(widened * widened, axis=-1, keepdims=True) + EPS_RMS)
        * norm_gain
    ).astype(jnp.bfloat16)
    proj_qkv = jnp.einsum("td,ide->ite", normed, wqkv, preferred_element_type=jnp.float32)
    q_part = proj_qkv[0]
    k_part = proj_qkv[1]
    v_part = proj_qkv[2]
    square_sums = lax.psum(
        (jnp.sum(q_part * q_part, axis=-1), jnp.sum(k_part * k_part, axis=-1)), "tp"
    )
    inner_width = HEADS * HD
    q_scaled = (
        q_part * lax.rsqrt(square_sums[0] / inner_width + EPS_RMS)[:, None] * qk_gain[0]
    ).astype(jnp.bfloat16)
    k_scaled = (
        k_part * lax.rsqrt(square_sums[1] / inner_width + EPS_RMS)[:, None] * qk_gain[1]
    ).astype(jnp.bfloat16)
    v_scaled = v_part.astype(jnp.bfloat16)
    heads_here = q_part.shape[1] // HD

    def split_heads(matrix):
        return matrix.reshape(seq_len, heads_here, HD).transpose(1, 0, 2)

    block_total = block_count(seq_len)
    block_rows = seq_len // block_total
    query_blocks = (
        split_heads(q_scaled).reshape(heads_here, block_total, block_rows, HD).transpose(1, 0, 2, 3)
    )
    seg_blocks = group_segs.reshape(block_total, block_rows)
    key_heads = split_heads(k_scaled)
    value_heads = split_heads(v_scaled)
    mixed = lax.map(
        lambda block_item: attend_block(
            block_item[0], key_heads, value_heads, block_item[1], group_segs
        ),
        (query_blocks, seg_blocks),
    )
    attended = mixed.transpose(0, 2, 1, 3).reshape(seq_len, heads_here * HD)
    width_dev = bproj.shape[0]
    head_part = jnp.dot(attended, wproj, preferred_element_type=jnp.float32)
    attn_out = lax.psum_scatter(head_part, "tp", scatter_dimension=1, tiled=True)
    own_columns = lax.dynamic_slice_in_dim(gathered, tp_index * width_dev, width_dev, 1).astype(
        jnp.float32
    )
    stream = (own_columns + layer_scale * (attn_out + bproj)).astype(jnp.bfloat16)
    merged = merge_rows(stream).astype(jnp.float32)
    feature_total = 4 * D
    row_mean = lax.psum(jnp.sum(merged, axis=(1, 2)), "tp") / feature_total
    centered = merged - row_mean[:, None, None]
    row_var = lax.psum(jnp.sum(centered * centered, axis=(1, 2)), "tp") / feature_total
    normal_rows = (
        centered * lax.rsqrt(row_var + EPS_LN)[:, None, None] * ln_weight + ln_bias
    ).astype(jnp.bfloat16)
    merged_total = normal_rows.shape[0]
    flat_rows = normal_rows.reshape(merged_total, 4 * width_dev)
    flat_weight = w_merge.reshape(4 * width_dev, w_merge.shape[2])
    merged_dev = merged_total // tp_total
    own_rows = lax.psum_scatter(
        jnp.dot(flat_rows, flat_weight, preferred_element_type=jnp.float32),
        "tp",
        scatter_dimension=0,
        tiled=True,
    )
    first_tokens = merge_rows(group_segs.reshape(seq_len, 1))[:, 0, 0]
    own_first = lax.dynamic_slice_in_dim(first_tokens, tp_index * merged_dev, merged_dev, 0)
    live_rows = (own_first >= 0).astype(jnp.float32)
    out_rows = (jax.nn.gelu(own_rows + b_merge, approximate=False) * live_rows[:, None]).astype(
        jnp.bfloat16
    )
    capacity = (merged_dev + group_total - 1) // group_total + 1
    group_ids = jnp.arange(group_total, dtype=jnp.int32)
    slot_ids = jnp.arange(capacity, dtype=jnp.int32)
    mine_ids = lax.dynamic_index_in_dim(owners[:, :, 0], req_index, 0, keepdims=False)
    slot_rank = slot_ranks(mine_ids, group_total)
    selector = (mine_ids[None, None, :] == group_ids[:, None, None]) & (
        slot_rank[None, None, :] == slot_ids[None, :, None]
    )
    outgoing = jnp.einsum(
        "gcm,mf->gcf", selector.astype(jnp.bfloat16), out_rows, preferred_element_type=jnp.float32
    ).astype(jnp.bfloat16)
    incoming = lax.all_to_all(outgoing, "req", split_axis=0, concat_axis=0, tiled=True)
    return incoming.reshape(1, group_total, 1, capacity, incoming.shape[-1])


def solution(mesh):
    placed = (
        P("req", "tp", None),
        P("req", None),
        P(),
        P(None, None, "tp"),
        P(None, "tp"),
        P("tp", None),
        P("tp"),
        P("tp"),
        P(None, "tp"),
        P(None, "tp"),
        P(None, "tp", None),
        P(),
        P(None, "tp", None),
    )
    return jax.shard_map(
        per_device,
        mesh=mesh,
        in_specs=placed,
        out_specs=P("req", None, "tp", None, None),
        check_vma=False,
    )
```

profile of v0, /device:TPU:32, one launch (start us, length us, event | category | flops | bytes accessed | tf_op | source)
XLA Modules:
  0.0 501.9 jit_solution(13317107277440170521)
XLA Ops:
  6.5 0.0 copy-start
  6.5 0.0 all-gather.2.cloned.1.call-start
  6.5 0.7 all-gather.2.cloned.1.call-update
  7.3 0.0 copy-start.10
  7.3 0.0 reduce-scatter.3.cloned.1.call-start
  7.3 3.3 copy.44
  10.6 0.0 copy-done.7
  10.6 91.8 %all-gather.2.cloned.1.call-done = bf16[1,512,3200]{2,1,0:T(8,128)(2,1)} async-done(((bf16[1,32,3200]{2,1,0:T(8,128)(2,1)}), bf16[1,512,3200]{2,1,0:T(8,128)(2,1)}) %all-gather.2.cloned.1.call-update) | async-done | bytes 3276816 | tf_op jit(solution)/shard_map/all_gather | solution.py:71
  102.4 2.8 fusion
  105.2 0.0 copy-done.10
  105.2 0.1 copy-done.1
  105.3 1.7 fusion.3
  107.0 0.0 copy-start.2
  107.0 0.9 copy-done.2
  107.9 0.1 multiply_reduce_fusion.2
  107.9 39.8 %all-reduce = (f32[512]{0:T(512)S(1)}, f32[512]{0:T(512)S(1)}) all-reduce(f32[512]{0:T(512)S(1)} %get-tuple-element.16, f32[512]{0:T(512)S(1)} %get-tuple-element.15), channel_id=1, replica_groups=mesh['req'=16,'tp'=16] {'tp'}, use_global_device_ids=true, to_apply=%region_6.7 | all-reduce | flops 1024 | bytes 8192 | tf_op jit(solution)/shard_map/psum | solution.py:84
  147.7 0.0 copy-done.6
  147.8 1.5 fusion.111
  149.2 0.2 fusion.10
  149.4 0.0 copy-done
  149.4 5.0 %fusion.9 = f32[512,3200]{0,1:T(8,128)} fusion(bf16[128,3200]{1,0:T(8,128)(2,1)S(1)} %copy-done, f32[512,512]{0,1:T(8,128)S(1)} %get-tuple-element.30, f32[512]{0:T(512)S(1)} %fusion.10, f32[512]{0:T(512)S(1)} %get-tuple-element.29, f32[3,512,128]{1,2,0:T(8,128)} %bitcast.62), kind=kOutput, calls=%fused_computation.14 | convolution fusion | flops 487391232 | bytes 8556544 | tf_op jit(solution)/shard_map/dot_general | solution.py:116
  154.5 0.0 reduce-scatter.3.cloned.1.call-update
  154.5 0.0 copy-start.3
  154.5 0.0 copy-start.4
  154.5 0.0 reduce-scatter.5.cloned.1.call-start
  154.6 1.1 constant_dynamic-slice_fusion.1
  155.7 0.1 copy.52
  155.8 144.5 %reduce-scatter.3.cloned.1.call-done = f32[512,200]{0,1:T(8,128)} async-done(((f32[512,3200]{0,1:T(8,128)}), f32[512,200]{0,1:T(8,128)}) %reduce-scatter.3.cloned.1.call-update) | async-done | bytes 409616 | tf_op jit(solution)/shard_map/reduce_scatter | solution.py:117
  300.4 0.0 copy-done.8
  300.4 0.0 copy-done.9
  300.4 1.1 fusion.20
  301.5 0.2 copy.45
  301.7 0.3 reshape.176
  302.0 0.3 bitcast_reduce_fusion
  302.4 0.1 reduce_sum.74
  302.4 42.0 %psum.30 = f32[128]{0:T(128)S(1)} all-reduce(f32[128]{0:T(128)S(1)} %reduce_sum.74), channel_id=1, replica_groups=mesh['req'=16,'tp'=16] {'tp'}, use_global_device_ids=true, to_apply=%region_11.12 | all-reduce | flops 128 | bytes 1024 | tf_op jit(solution)/shard_map/psum | solution.py:124
  344.5 0.1 sub.36
  344.5 0.6 multiply_reduce_fusion
  345.2 0.1 reduce_sum.76
  345.2 39.2 %psum.31 = f32[128]{0:T(128)S(1)} all-reduce(f32[128]{0:T(128)S(1)} %reduce_sum.76), channel_id=1, replica_groups=mesh['req'=16,'tp'=16] {'tp'}, use_global_device_ids=true, to_apply=%region_13.14 | all-reduce | flops 128 | bytes 1024 | tf_op jit(solution)/shard_map/psum | solution.py:126
  384.4 0.1 copy.46
  384.5 0.0 copy-done.3
  384.5 0.0 copy-done.4
  384.5 0.0 copy-start.5
  384.5 0.0 copy-start.11
  384.6 4.7 convolution_bitcast_fusion
  389.2 0.0 reduce-scatter.5.cloned.1.call-update
  389.3 0.5 broadcast.123
  389.8 0.7 reduce.13
  390.4 0.0 copy-done.5
  390.4 0.3 dynamic-slice_reduce_fusion
  390.7 0.1 fusion.77
  390.8 0.1 reshape_reshape_squeeze.3
  391.0 0.2 copy.48
  391.2 0.1 reshape.169
  391.2 0.1 fusion.80
  391.3 0.2 select_reduce_fusion
  391.5 0.1 iota_compare_fusion.1
  391.6 81.3 %reduce-scatter.5.cloned.1.call-done = f32[8,3072]{1,0:T(8,128)} async-done(((f32[128,3072]{1,0:T(8,128)}), f32[8,3072]{1,0:T(8,128)}) %reduce-scatter.5.cloned.1.call-update) | async-done | bytes 98320 | tf_op jit(solution)/shard_map/reduce_scatter | solution.py:134
  472.9 0.0 copy-done.11
  472.9 1.3 convolution_convert_fusion
  474.2 0.2 copy.49
  474.4 20.3 %all_to_all.5 = bf16[16,2,3072]{2,1,0:T(2,128)(2,1)S(1)} all-to-all(bf16[16,2,3072]{2,1,0:T(2,128)(2,1)S(1)} %copy.49), channel_id=1, replica_groups=mesh['req'=16,'tp'=16] {'req'}, dimensions={0} | all-to-all | bytes 393216 | tf_op jit(solution)/shard_map/all_to_all | solution.py:157
  494.7 0.7 copy.54
  (13 shorter events, 0.1 us)
Async XLA Ops:
  6.5 142.9 %copy-start = (bf16[128,3200]{1,0:T(8,128)(2,1)S(1)}, bf16[128,3200]{1,0:T(8,128)(2,1)}, u32[]{:S(2)}) copy-start(bf16[128,3200]{1,0:T(8,128)(2,1)} %param.18) | copy-start | bytes 2457604
  6.5 4.1 copy-start.7
  6.5 95.9 %all-gather.2.cloned.1.call-start = ((), (), s32[]{:S(2)}) async-start(), calls=%async_computation.3 | async-start | bytes 3481600 | tf_op jit(solution)/shard_map/all_gather | solution.py:71
  7.3 97.9 %copy-start.10 = (f32[3200]{0:T(1024)S(1)}, f32[3200]{0:T(1024)}, u32[]{:S(2)}) copy-start(f32[3200]{0:T(1024)} %param.15) | copy-start | bytes 38404
  7.3 293.1 %reduce-scatter.3.cloned.1.call-start = ((), (), s32[]{:S(2)}) async-start(), calls=%async_computation.4 | async-start | bytes 6963200 | tf_op jit(solution)/shard_map/reduce_scatter | solution.py:117
  102.4 2.9 copy-start.1
  105.3 42.4 %copy-start.6 = (s32[1,512]{1,0:T(1,128)S(1)}, s32[1,512]{1,0:T(1,128)}, u32[]{:S(2)}) copy-start(s32[1,512]{1,0:T(1,128)} %param.14) | copy-start | bytes 6148
  107.0 0.9 copy-start.2
  154.5 145.9 %copy-start.8 = (f32[200]{0:T(256)S(1)}, f32[200]{0:T(256)}, u32[]{:S(2)}) copy-start(f32[200]{0:T(256)} %param.19) | copy-start | bytes 2404
  154.5 145.9 %copy-start.9 = (f32[200]{0:T(256)S(1)}, f32[200]{0:T(256)}, u32[]{:S(2)}) copy-start(f32[200]{0:T(256)} %param.20) | copy-start | bytes 2404
  154.5 230.0 %copy-start.3 = (f32[4,200]{1,0:T(4,128)S(1)}, f32[4,200]{1,0:T(4,128)}, u32[]{:S(2)}) copy-start(f32[4,200]{1,0:T(4,128)} %param.22) | copy-start | bytes 9604
  154.5 230.0 %copy-start.4 = (f32[4,200]{1,0:T(4,128)S(1)}, f32[4,200]{1,0:T(4,128)}, u32[]{:S(2)}) copy-start(f32[4,200]{1,0:T(4,128)} %param.21) | copy-start | bytes 9604
  154.5 318.4 %reduce-scatter.5.cloned.1.call-start = ((), (), s32[]{:S(2)}) async-start(), calls=%async_computation.5 | async-start | bytes 1671168 | tf_op jit(solution)/shard_map/reduce_scatter | solution.py:134
  384.5 5.9 %copy-start.5 = (s32[16,8,1]{0,2,1:T(1,128)S(1)}, s32[16,8,1]{0,2,1:T(1,128)}, u32[]{:S(2)}) copy-start(s32[16,8,1]{0,2,1:T(1,128)} %param.25) | copy-start | bytes 1540
  384.5 88.3 %copy-start.11 = (f32[3072]{0:T(1024)S(1)}, f32[3072]{0:T(1024)}, u32[]{:S(2)}) copy-start(f32[3072]{0:T(1024)} %param.24) | copy-start | bytes 36868
Sparse Core Ops, SparseCore 0:
  9.1 93.2 all-gather.1
  154.6 145.7 reduce-scatter.2
  389.4 83.4 reduce-scatter.4
where the time goes:
time: 506 us; the launch traced here: 502 us
  waiting for transfers between devices  318 us (63%)
  blocking collectives  141 us (28%)
  matrix products  14.1 us (3%)
  between operations  13.3 us (3%)
  local copies, waits for them, and re-layouts  8.46 us (2%)
  other arithmetic  6.28 us (1%)
    reduce_scatter x1, waiting for transfers between devices, per_device(): lax.psum_scatter(head_part, 'tp', scatter_dimension=1, tiled=True)  145 us
    all_gather x1, waiting for transfers between devices, per_device(): gathered = lax.all_gather(tokens, 'tp', axis=1, tiled=True)[0]  91.8 us
    reduce_scatter x1, waiting for transfers between devices, per_device(): lax.psum_scatter(jnp.dot(flat_rows, flat_weight, preferred_element_type=j...  81.3 us
    psum x1, blocking collectives, per_device(): row_mean = lax.psum(jnp.sum(merged, axis=(1, 2)), 'tp') / feature_total  42 us
    psum x1, blocking collectives, per_device(): lax.psum((jnp.sum(q_part * q_part, axis=-1), jnp.sum(k_part * k_part, axi...  39.8 us
    psum x1, blocking collectives, per_device(): lax.psum(jnp.sum(centered * centered, axis=(1, 2)), 'tp') / feature_total  39.2 us
    all_to_all x1, blocking collectives, per_device(): lax.all_to_all(outgoing, 'req', split_axis=0, concat_axis=0, tiled=True)  20.3 us
  transfers between devices with their start and end apart: 3, of which 3 were waited for; matrix products, arithmetic and copies ran while one was open for 1% of the time, Pallas kernels for 0%

commit v1 on v0

--- a/solution.py
+++ b/solution.py
@@ -1,6 +1,7 @@
 import jax
 import jax.numpy as jnp
 from jax import lax
+from jax.sharding import Mesh
 from jax.sharding import PartitionSpec as P
 
 D = 3200
@@ -11,6 +12,8 @@
 
 EPS_RMS = 1e-06
 EPS_LN = 1e-05
+
+TP_AXES = ("ty", "tz")
 
 
 def block_count(length):
@@ -47,6 +50,16 @@
     )
     before = jnp.cumsum(owner_hits, axis=0) - owner_hits
     return jnp.sum(before * owner_hits, axis=1)
+
+
+def tp_gather(value, axis):
+    inner = lax.all_gather(value, "tz", axis=axis, tiled=True)
+    return lax.all_gather(inner, "ty", axis=axis, tiled=True)
+
+
+def tp_scatter_sum(value, axis):
+    outer = lax.psum_scatter(value, "ty", scatter_dimension=axis, tiled=True)
+    return lax.psum_scatter(outer, "tz", scatter_dimension=axis, tiled=True)
 
 
 def per_device(
@@ -64,11 +77,11 @@
     b_merge,
     owners,
 ):
-    tp_total = lax.axis_size("tp")
-    tp_index = lax.axis_index("tp")
+    tp_total = lax.axis_size("ty") * lax.axis_size("tz")
+    tp_index = lax.axis_index("ty") * lax.axis_size("tz") + lax.axis_index("tz")
     req_index = lax.axis_index("req")
     group_total = lax.axis_size("req")
-    gathered = lax.all_gather(tokens, "tp", axis=1, tiled=True)[0]
+    gathered = tp_gather(tokens, 1)[0]
     seq_len = gathered.shape[0]
     group_segs = segments[0]
     widened = gathered.astype(jnp.float32)
@@ -82,7 +95,7 @@
     k_part = proj_qkv[1]
     v_part = proj_qkv[2]
     square_sums = lax.psum(
-        (jnp.sum(q_part * q_part, axis=-1), jnp.sum(k_part * k_part, axis=-1)), "tp"
+        (jnp.sum(q_part * q_part, axis=-1), jnp.sum(k_part * k_part, axis=-1)), TP_AXES
     )
     inner_width = HEADS * HD
     q_scaled = (
@@ -114,16 +127,24 @@
     attended = mixed.transpose(0, 2, 1, 3).reshape(seq_len, heads_here * HD)
     width_dev = bproj.shape[0]
     head_part = jnp.dot(attended, wproj, preferred_element_type=jnp.float32)
-    attn_out = lax.psum_scatter(head_part, "tp", scatter_dimension=1, tiled=True)
+    attn_out = tp_scatter_sum(head_part.astype(jnp.bfloat16), 1).astype(jnp.float32)
     own_columns = lax.dynamic_slice_in_dim(gathered, tp_index * width_dev, width_dev, 1).astype(
         jnp.float32
     )
     stream = (own_columns + layer_scale * (attn_out + bproj)).astype(jnp.bfloat16)
     merged = merge_rows(stream).astype(jnp.float32)
     feature_total = 4 * D
-    row_mean = lax.psum(jnp.sum(merged, axis=(1, 2)), "tp") / feature_total
+    local_count = 4 * width_dev
+    local_sum = jnp.sum(merged, axis=(1, 2))
+    local_mean = local_sum / local_count
+    local_dev = merged - local_mean[:, None, None]
+    local_m2 = jnp.sum(local_dev * local_dev, axis=(1, 2))
+    stats = lax.all_gather(jnp.stack([local_sum, local_m2]), TP_AXES, axis=0, tiled=False)
+    row_mean = jnp.sum(stats[:, 0], axis=0) / feature_total
+    spread = stats[:, 0] / local_count - row_mean[None, :]
+    row_m2 = jnp.sum(stats[:, 1], axis=0) + local_count * jnp.sum(spread * spread, axis=0)
+    row_var = row_m2 / feature_total
     centered = merged - row_mean[:, None, None]
-    row_var = lax.psum(jnp.sum(centered * centered, axis=(1, 2)), "tp") / feature_total
     normal_rows = (
         centered * lax.rsqrt(row_var + EPS_LN)[:, None, None] * ln_weight + ln_bias
     ).astype(jnp.bfloat16)
@@ -131,12 +152,10 @@
     flat_rows = normal_rows.reshape(merged_total, 4 * width_dev)
     flat_weight = w_merge.reshape(4 * width_dev, w_merge.shape[2])
     merged_dev = merged_total // tp_total
-    own_rows = lax.psum_scatter(
-        jnp.dot(flat_rows, flat_weight, preferred_element_type=jnp.float32),
-        "tp",
-        scatter_dimension=0,
-        tiled=True,
-    )
+    own_rows = tp_scatter_sum(
+        jnp.dot(flat_rows, flat_weight, preferred_element_type=jnp.float32).astype(jnp.bfloat16),
+        0,
+    ).astype(jnp.float32)
     first_tokens = merge_rows(group_segs.reshape(seq_len, 1))[:, 0, 0]
     own_first = lax.dynamic_slice_in_dim(first_tokens, tp_index * merged_dev, merged_dev, 0)
     live_rows = (own_first >= 0).astype(jnp.float32)
@@ -159,25 +178,31 @@
 
 
 def solution(mesh):
+    grid = mesh.devices
+    inner = 4 if grid.shape[1] % 4 == 0 else 1
+    split = Mesh(
+        grid.reshape(grid.shape[0], grid.shape[1] // inner, inner), ("req",) + TP_AXES
+    )
+    tp = TP_AXES
     placed = (
-        P("req", "tp", None),
+        P("req", tp, None),
         P("req", None),
         P(),
-        P(None, None, "tp"),
-        P(None, "tp"),
-        P("tp", None),
-        P("tp"),
-        P("tp"),
-        P(None, "tp"),
-        P(None, "tp"),
-        P(None, "tp", None),
+        P(None, None, tp),
+        P(None, tp),
+        P(tp, None),
+        P(tp),
+        P(tp),
+        P(None, tp),
+        P(None, tp),
+        P(None, tp, None),
         P(),
-        P(None, "tp", None),
+        P(None, tp, None),
     )
     return jax.shard_map(
         per_device,
-        mesh=mesh,
+        mesh=split,
         in_specs=placed,
-        out_specs=P("req", None, "tp", None, None),
+        out_specs=P("req", None, tp, None, None),
         check_vma=False,
     )

time: 506 us -> 326 us (0.64)
  waiting for transfers between devices: 318 us -> 166 us
  blocking collectives: 141 us -> 119 us
    reduce_scatter x2 -> x4, waiting for transfers between devices: 226 us -> 120 us  [the longest x2 66.9 us: tp_scatter_sum(): outer = lax.psum_scatter(value, 'ty', scatter_dimension=axis, tiled=True)]
    psum x2 -> x0, blocking collectives: 81.2 us -> none  [the longest x1 42 us: per_device(): row_mean = lax.psum(jnp.sum(merged, axis=(1, 2)), 'tp') / feature_total]
    all_gather x0 -> x2, blocking collectives: none -> 58.3 us  [the longest x1 39.1 us: per_device(): lax.all_gather(jnp.stack([local_sum, local_m2]), TP_AXES, axis=0, tiled=F...]
    all_gather x1, waiting for transfers between devices: 91.8 us -> 45.3 us  [tp_gather(): return lax.all_gather(inner, 'ty', axis=axis, tiled=True)]
  transfers between devices with their start and end apart: 3 -> 5, of which waited for: 3 -> 5; matrix products, arithmetic and copies ran while one was open for 1% -> 2% of each run, Pallas kernels for 0% -> 0%
where the time goes in v1:
time: 326 us
  waiting for transfers between devices  166 us (51%)
  blocking collectives  119 us (37%)
  between operations  13.4 us (4%)
  matrix products  12.7 us (4%)
  local copies, waits for them, and re-layouts  8.38 us (3%)
  other arithmetic  6.44 us (2%)
    reduce_scatter x2, waiting for transfers between devices, tp_scatter_sum(): outer = lax.psum_scatter(value, 'ty', scatter_dimension=axis, tiled=True)  66.9 us
    reduce_scatter x2, waiting for transfers between devices, tp_scatter_sum(): return lax.psum_scatter(outer, 'tz', scatter_dimension=axis, tiled=True)  53.4 us
    all_gather x1, waiting for transfers between devices, tp_gather(): return lax.all_gather(inner, 'ty', axis=axis, tiled=True)  45.3 us
    all_gather x1, blocking collectives, per_device(): lax.all_gather(jnp.stack([local_sum, local_m2]), TP_AXES, axis=0, tiled=F...  39.1 us
    psum x1, blocking collectives, per_device(): lax.psum((jnp.sum(q_part * q_part, axis=-1), jnp.sum(k_part * k_part, axi...  38.4 us
    all_to_all x1, blocking collectives, per_device(): lax.all_to_all(outgoing, 'req', split_axis=0, concat_axis=0, tiled=True)  22.4 us
    all_gather x1, blocking collectives, tp_gather(): inner = lax.all_gather(value, 'tz', axis=axis, tiled=True)  19.2 us
  transfers between devices with their start and end apart: 5, of which 5 were waited for; matrix products, arithmetic and copies ran while one was open for 2% of the time, Pallas kernels for 0%

profile of v1, /device:TPU:32, one launch (start us, length us, event | category | flops | bytes accessed | tf_op | source)
XLA Modules:
  0.0 325.9 jit_solution(5453652894021176367)
XLA Ops:
  6.5 0.0 copy-start
  6.5 0.0 all-gather.4.cloned.1.call-start
  6.5 19.2 %all_gather.12 = bf16[1,128,3200]{2,1,0:T(8,128)(2,1)S(1)} all-gather(bf16[1,32,3200]{2,1,0:T(8,128)(2,1)} %param.13), channel_id=1, replica_groups=mesh['req'=16,'ty'=4,'tz'=4] {'tz'}, dimensions={1}, use_global_device_ids=true | all-gather | bytes 1024000 | tf_op jit(solution)/shard_map/all_gather | solution.py:56
  25.8 1.3 copy.44
  27.1 0.0 all-gather.4.cloned.1.call-update
  27.1 0.0 copy-start.10
  27.1 0.0 reduce-scatter.5.cloned.1.call-start
  27.2 3.3 %copy.46 = bf16[3,3200,128]{1,2,0:T(8,128)(2,1)S(1)} copy(bf16[3,3200,128]{2,1,0:T(8,128)(2,1)} %param.16) | data formatting | bytes 4915200 | tf_op args[3]
  30.4 0.0 copy-done.9
  30.5 45.3 %all-gather.4.cloned.1.call-done = bf16[1,512,3200]{1,2,0:T(8,128)(2,1)} async-done(((bf16[1,128,3200]{1,2,0:T(8,128)(2,1)}), bf16[1,512,3200]{1,2,0:T(8,128)(2,1)}) %all-gather.4.cloned.1.call-update) | async-done | bytes 3276816 | tf_op jit(solution)/shard_map/all_gather | solution.py:57
  75.8 2.8 fusion
  78.6 0.0 copy-done.10
  78.6 0.1 copy-done.1
  78.7 1.6 fusion.4
  80.3 0.0 copy-start.2
  80.3 0.9 copy-done.2
  81.2 0.1 multiply_reduce_fusion.2
  81.3 38.4 %all-reduce = (f32[512]{0:T(512)S(1)}, f32[512]{0:T(512)S(1)}) all-reduce(f32[512]{0:T(512)S(1)} %get-tuple-element.16, f32[512]{0:T(512)S(1)} %get-tuple-element.15), channel_id=1, replica_groups=mesh['req'=16,'ty'=4,'tz'=4] {'ty','tz'}, use_global_device_ids=true, to_apply=%region_6.7 | all-reduce | flops 1024 | bytes 8192 | tf_op jit(solution)/shard_map/psum | solution.py:97
  119.7 0.0 copy-done.6
  119.7 1.5 fusion.115
  121.2 0.2 fusion.10
  121.4 4.0 %convolution_convert_fusion = bf16[512,3200]{0,1:T(8,128)(2,1)} fusion(bf16[128,3200]{1,0:T(8,128)(2,1)S(1)} %copy-done, f32[512,512]{0,1:T(8,128)S(1)} %get-tuple-element.33, f32[512]{0:T(512)S(1)} %fusion.10, f32[512]{0:T(512)S(1)} %get-tuple-element.32, f32[3,512,128]{1,2,0:T(8,128)} %bitcast.69), kind=kOutput, calls=%fused_computation.5 | convolution fusion | flops 489029632 | bytes 5279744 | tf_op jit(solution)/shard_map/dot_general | solution.py:129
  125.4 0.0 reduce-scatter.5.cloned.1.call-update
  125.4 0.0 copy-start.3
  125.4 0.0 copy-start.4
  125.4 0.0 reduce-scatter.7.cloned.1.call-start
  125.5 42.7 %reduce-scatter.5.cloned.1.call-done = bf16[512,800]{0,1:T(8,128)(2,1)} async-done(((bf16[512,3200]{0,1:T(8,128)(2,1)}), bf16[512,800]{0,1:T(8,128)(2,1)}) %reduce-scatter.5.cloned.1.call-update) | async-done | bytes 819216 | tf_op jit(solution)/shard_map/reduce_scatter | solution.py:61
  168.2 0.0 reduce-scatter.7.cloned.1.call-update
  168.3 0.0 reduce-scatter.9.cloned.1.call-start
  168.3 29.4 %reduce-scatter.7.cloned.1.call-done = bf16[512,200]{0,1:T(8,128)(2,1)} async-done(((bf16[512,800]{0,1:T(8,128)(2,1)}), bf16[512,200]{0,1:T(8,128)(2,1)}) %reduce-scatter.7.cloned.1.call-update) | async-done | bytes 204816 | tf_op jit(solution)/shard_map/reduce_scatter | solution.py:62
  197.7 0.0 copy-done.7
  197.7 1.2 fusion.20
  198.9 0.2 copy.47
  199.1 0.3 reshape.199
  199.4 0.3 bitcast_reduce_fusion
  199.8 0.1 stack.9
  199.8 0.6 multiply_reduce_fusion
  200.5 0.1 stack.10
  200.6 39.1 %all-gather.1 = f32[16,2,128]{2,1,0:T(2,128)S(1)} all-gather(f32[1,2,128]{2,1,0:T(2,128)S(1)} %maximum_bitcast_fusion), channel_id=2, replica_groups=mesh['req'=16,'ty'=4,'tz'=4] {'ty','tz'}, dimensions={0}, use_global_device_ids=true | all-gather | bytes 17408 | tf_op jit(solution)/shard_map/all_gather | solution.py:142
  239.7 0.1 copy.48
  239.8 0.0 copy-done.3
  239.8 0.0 copy-done.4
  239.8 0.0 copy-start.5
  239.8 0.0 copy-start.11
  239.8 4.4 %fusion.3 = bf16[128,3072]{1,0:T(8,128)(2,1)} fusion(bf16[4,200,3072]{2,1,0:T(8,128)(2,1)} %param.23, f32[128,4,200]{2,0,1:T(8,128)S(1)} %bitcast.64, f32[4,200]{1,0:T(4,128)S(1)} %copy-done.3, f32[4,200]{1,0:T(4,128)S(1)} %copy-done.4, f32[128]{0:T(128)S(1)} %add_rsqrt_fusion.3, f32[128]{0:T(128)S(1)} %broadcast_multiply_fusion.1), kind=kOutput, calls=%fused_computation.7 | convolution fusion | flops 630050816 | bytes 6118656 | tf_op jit(solution)/shard_map/dot_general | solution.py:156
  244.2 0.0 reduce-scatter.9.cloned.1.call-update
  244.2 0.0 reduce-scatter.11.cloned.1.call-start
  244.3 0.3 dynamic-slice_reduce_fusion
  244.6 0.1 fusion.81
  244.7 0.5 broadcast.158
  245.2 0.7 reduce.15
  245.9 0.1 reshape_reshape_squeeze.3
  246.0 0.2 copy.50
  246.2 0.1 reshape.192
  246.3 0.1 fusion.84
  246.3 0.2 select_reduce_fusion
  246.5 24.2 %reduce-scatter.9.cloned.1.call-done = bf16[32,3072]{1,0:T(8,128)(2,1)} async-done(((bf16[128,3072]{1,0:T(8,128)(2,1)}), bf16[32,3072]{1,0:T(8,128)(2,1)}) %reduce-scatter.9.cloned.1.call-update) | async-done | bytes 196624 | tf_op jit(solution)/shard_map/reduce_scatter | solution.py:61
  270.7 0.0 reduce-scatter.11.cloned.1.call-update
  270.7 0.1 iota_compare_fusion.1
  270.8 24.0 %reduce-scatter.11.cloned.1.call-done = bf16[8,3072]{1,0:T(8,128)(2,1)} async-done(((bf16[32,3072]{1,0:T(8,128)(2,1)}), bf16[8,3072]{1,0:T(8,128)(2,1)}) %reduce-scatter.11.cloned.1.call-update) | async-done | bytes 49168 | tf_op jit(solution)/shard_map/reduce_scatter | solution.py:62
  294.8 1.2 convolution_convert_fusion.1
  296.1 0.2 copy.51
  296.3 22.4 %all_to_all.5 = bf16[16,2,3072]{2,1,0:T(2,128)(2,1)S(1)} all-to-all(bf16[16,2,3072]{2,1,0:T(2,128)(2,1)S(1)} %copy.51), channel_id=1, replica_groups=mesh['req'=16,'ty'=4,'tz'=4] {'req'}, dimensions={0} | all-to-all | bytes 393216 | tf_op jit(solution)/shard_map/all_to_all | solution.py:176
  318.7 0.7 copy.56
  (21 shorter events, 0.2 us)
Async XLA Ops:
  6.5 114.8 %copy-start = (bf16[128,3200]{1,0:T(8,128)(2,1)S(1)}, bf16[128,3200]{1,0:T(8,128)(2,1)}, u32[]{:S(2)}) copy-start(bf16[128,3200]{1,0:T(8,128)(2,1)} %param.18) | copy-start | bytes 2457604
  6.5 69.2 %all-gather.4.cloned.1.call-start = ((), (), s32[]{:S(2)}) async-start(), calls=%async_computation.5 | async-start | bytes 4096000 | tf_op jit(solution)/shard_map/all_gather | solution.py:57
  27.1 3.4 %copy-start.9 = (f32[2,128]{1,0:T(2,128)S(1)}, f32[2,128]{1,0:T(2,128)}, u32[]{:S(2)}) copy-start(f32[2,128]{1,0:T(2,128)} %param.17) | copy-start | bytes 3076
  27.1 51.5 %copy-start.10 = (f32[3200]{0:T(1024)S(1)}, f32[3200]{0:T(1024)}, u32[]{:S(2)}) copy-start(f32[3200]{0:T(1024)} %param.15) | copy-start | bytes 38404
  27.1 141.1 %reduce-scatter.5.cloned.1.call-start = ((), (), s32[]{:S(2)}) async-start(), calls=%async_computation.6 | async-start | bytes 4096000 | tf_op jit(solution)/shard_map/reduce_scatter | solution.py:61
  75.8 2.9 copy-start.1
  78.7 41.0 %copy-start.6 = (s32[1,512]{1,0:T(1,128)S(1)}, s32[1,512]{1,0:T(1,128)}, u32[]{:S(2)}) copy-start(s32[1,512]{1,0:T(1,128)} %param.14) | copy-start | bytes 6148
  80.3 0.9 copy-start.2
  125.4 72.3 %copy-start.7 = (f32[200]{0:T(256)S(1)}, f32[200]{0:T(256)}, u32[]{:S(2)}) copy-start(f32[200]{0:T(256)} %param.19) | copy-start | bytes 2404
  125.4 72.3 %copy-start.8 = (f32[200]{0:T(256)S(1)}, f32[200]{0:T(256)}, u32[]{:S(2)}) copy-start(f32[200]{0:T(256)} %param.20) | copy-start | bytes 2404
  125.4 114.4 %copy-start.3 = (f32[4,200]{1,0:T(4,128)S(1)}, f32[4,200]{1,0:T(4,128)}, u32[]{:S(2)}) copy-start(f32[4,200]{1,0:T(4,128)} %param.22) | copy-start | bytes 9604
  125.4 114.4 %copy-start.4 = (f32[4,200]{1,0:T(4,128)S(1)}, f32[4,200]{1,0:T(4,128)}, u32[]{:S(2)}) copy-start(f32[4,200]{1,0:T(4,128)} %param.21) | copy-start | bytes 9604
  125.4 72.3 %reduce-scatter.7.cloned.1.call-start = ((), (), s32[]{:S(2)}) async-start(), calls=%async_computation.7 | async-start | bytes 1024000 | tf_op jit(solution)/shard_map/reduce_scatter | solution.py:62
  168.3 102.5 %reduce-scatter.9.cloned.1.call-start = ((), (), s32[]{:S(2)}) async-start(), calls=%async_computation.8 | async-start | bytes 983040 | tf_op jit(solution)/shard_map/reduce_scatter | solution.py:61
  239.8 4.5 %copy-start.5 = (s32[16,8,1]{0,2,1:T(1,128)S(1)}, s32[16,8,1]{0,2,1:T(1,128)}, u32[]{:S(2)}) copy-start(s32[16,8,1]{0,2,1:T(1,128)} %param.25) | copy-start | bytes 1540
  239.8 55.0 %copy-start.11 = (f32[3072]{0:T(1024)S(1)}, f32[3072]{0:T(1024)}, u32[]{:S(2)}) copy-start(f32[3072]{0:T(1024)} %param.24) | copy-start | bytes 36868
  244.2 50.6 %reduce-scatter.11.cloned.1.call-start = ((), (), s32[]{:S(2)}) async-start(), calls=%async_computation.9 | async-start | bytes 245760 | tf_op jit(solution)/shard_map/reduce_scatter | solution.py:62
Sparse Core Ops, SparseCore 0:
  27.2 48.5 all-gather.3
  125.5 42.6 reduce-scatter.4
  170.8 26.8 reduce-scatter.6
  244.3 26.3 reduce-scatter.8
  273.1 21.7 reduce-scatter.10

commit v2 on v1

--- a/solution.py
+++ b/solution.py
@@ -60,6 +60,26 @@
 def tp_scatter_sum(value, axis):
     outer = lax.psum_scatter(value, "ty", scatter_dimension=axis, tiled=True)
     return lax.psum_scatter(outer, "tz", scatter_dimension=axis, tiled=True)
+
+
+def scatter_sum_exchange(value, axis_name, axis):
+    count = lax.axis_size(axis_name)
+    shape = value.shape
+    parts = value.reshape(shape[:axis] + (count, shape[axis] // count) + shape[axis + 1 :])
+    got = lax.all_to_all(parts, axis_name, split_axis=axis, concat_axis=axis, tiled=True)
+    return jnp.sum(got.astype(jnp.float32), axis=axis)
+
+
+def butterfly_gather(value):
+    out = value
+    for axis_name in ("tz", "ty"):
+        count = lax.axis_size(axis_name)
+        step = 1
+        while step < count:
+            swap = [(i, i ^ step) for i in range(count)]
+            out = jnp.concatenate([out, lax.ppermute(out, axis_name, swap)], axis=0)
+            step = step * 2
+    return out
 
 
 def per_device(
@@ -95,7 +115,8 @@
     k_part = proj_qkv[1]
     v_part = proj_qkv[2]
     square_sums = lax.psum(
-        (jnp.sum(q_part * q_part, axis=-1), jnp.sum(k_part * k_part, axis=-1)), TP_AXES
+        lax.psum(jnp.stack([jnp.sum(q_part * q_part, axis=-1), jnp.sum(k_part * k_part, axis=-1)]), "tz"),
+        "ty",
     )
     inner_width = HEADS * HD
     q_scaled = (
@@ -127,7 +148,8 @@
     attended = mixed.transpose(0, 2, 1, 3).reshape(seq_len, heads_here * HD)
     width_dev = bproj.shape[0]
     head_part = jnp.dot(attended, wproj, preferred_element_type=jnp.float32)
-    attn_out = tp_scatter_sum(head_part.astype(jnp.bfloat16), 1).astype(jnp.float32)
+    attn_outer = lax.psum_scatter(head_part.astype(jnp.bfloat16), "ty", scatter_dimension=1, tiled=True)
+    attn_out = scatter_sum_exchange(attn_outer, "tz", 1)
     own_columns = lax.dynamic_slice_in_dim(gathered, tp_index * width_dev, width_dev, 1).astype(
         jnp.float32
     )
@@ -139,7 +161,7 @@
     local_mean = local_sum / local_count
     local_dev = merged - local_mean[:, None, None]
     local_m2 = jnp.sum(local_dev * local_dev, axis=(1, 2))
-    stats = lax.all_gather(jnp.stack([local_sum, local_m2]), TP_AXES, axis=0, tiled=False)
+    stats = butterfly_gather(jnp.stack([local_sum, local_m2])[None])
     row_mean = jnp.sum(stats[:, 0], axis=0) / feature_total
     spread = stats[:, 0] / local_count - row_mean[None, :]
     row_m2 = jnp.sum(stats[:, 1], axis=0) + local_count * jnp.sum(spread * spread, axis=0)

time: 326 us -> 271 us (0.83)
  blocking collectives: 119 us -> 60 us
  starting transfers between devices: 0.16 us -> 12.5 us
  waiting for transfers between devices: 166 us -> 158 us
    reduce_scatter x2 -> x1, waiting for transfers between devices: 66.9 us -> 23.3 us  [tp_scatter_sum(): outer = lax.psum_scatter(value, 'ty', scatter_dimension=axis, tiled=True)]
    reduce_scatter x0 -> x1, waiting for transfers between devices: none -> 41.6 us  [per_device(): lax.psum_scatter(head_part.astype(jnp.bfloat16), 'ty', scatter_dimension=...]
    all_gather x1 -> x0, blocking collectives: 39.1 us -> none  [per_device(): lax.all_gather(jnp.stack([local_sum, local_m2]), TP_AXES, axis=0, tiled=F...]
    reduce_scatter x2 -> x1, waiting for transfers between devices: 53.4 us -> 24 us  [tp_scatter_sum(): return lax.psum_scatter(outer, 'tz', scatter_dimension=axis, tiled=True)]
    psum x1 -> x2, blocking collectives: 38.4 us -> 17.7 us  [the longest x1 8.98 us: per_device(): lax.psum(jnp.stack([jnp.sum(q_part * q_part, axis=-1), jnp.sum(k_part * k...]
    all_to_all x0 -> x1, waiting for transfers between devices: none -> 16 us  [scatter_sum_exchange(): lax.all_to_all(parts, axis_name, split_axis=axis, concat_axis=axis, tiled...]
    ppermute x0 -> x4, waiting for transfers between devices: none -> 11 us  [butterfly_gather(): out = jnp.concatenate([out, lax.ppermute(out, axis_name, swap)], axis=0)]
    ppermute x0 -> x4, starting transfers between devices: none -> 7.06 us  [butterfly_gather(): out = jnp.concatenate([out, lax.ppermute(out, axis_name, swap)], axis=0)]
  transfers between devices with their start and end apart: 5 -> 9, of which waited for: 5 -> 9; matrix products, arithmetic and copies ran while one was open for 2% -> 3% of each run, Pallas kernels for 0% -> 0%
where the time goes in v2:
time: 271 us
  waiting for transfers between devices  158 us (58%)
  blocking collectives  60 us (22%)
  between operations  13.4 us (5%)
  matrix products  12.8 us (5%)
  starting transfers between devices  12.5 us (5%)
  local copies, waits for them, and re-layouts  7.48 us (3%)
  other arithmetic  6.75 us (2%)
    all_gather x1, waiting for transfers between devices, tp_gather(): return lax.all_gather(inner, 'ty', axis=axis, tiled=True)  41.9 us
    reduce_scatter x1, waiting for transfers between devices, per_device(): lax.psum_scatter(head_part.astype(jnp.bfloat16), 'ty', scatter_dimension=...  41.6 us
    reduce_scatter x1, waiting for transfers between devices, tp_scatter_sum(): return lax.psum_scatter(outer, 'tz', scatter_dimension=axis, tiled=True)  24 us
    reduce_scatter x1, waiting for transfers between devices, tp_scatter_sum(): outer = lax.psum_scatter(value, 'ty', scatter_dimension=axis, tiled=True)  23.3 us
    all_to_all x1, blocking collectives, per_device(): lax.all_to_all(outgoing, 'req', split_axis=0, concat_axis=0, tiled=True)  22.4 us
    all_gather x1, blocking collectives, tp_gather(): inner = lax.all_gather(value, 'tz', axis=axis, tiled=True)  19.9 us
    all_to_all x1, waiting for transfers between devices, scatter_sum_exchange(): lax.all_to_all(parts, axis_name, split_axis=axis, concat_axis=axis, tiled...  16 us
    ppermute x4, waiting for transfers between devices, butterfly_gather(): out = jnp.concatenate([out, lax.ppermute(out, axis_name, swap)], axis=0)  11 us
  transfers between devices with their start and end apart: 9, of which 9 were waited for; matrix products, arithmetic and copies ran while one was open for 3% of the time, Pallas kernels for 0%

profile of v2, /device:TPU:32, one launch (start us, length us, event | category | flops | bytes accessed | tf_op | source)
XLA Modules:
  0.0 270.9 jit_solution(8555819555745562921)
XLA Ops:
  6.5 0.0 all-gather.2.cloned.1.call-start
  6.5 19.9 %all_gather.6 = bf16[1,128,3200]{2,1,0:T(8,128)(2,1)} all-gather(bf16[1,32,3200]{2,1,0:T(8,128)(2,1)} %param.13), channel_id=1, replica_groups=mesh['req'=16,'ty'=4,'tz'=4] {'tz'}, dimensions={1}, use_global_device_ids=true | all-gather | bytes 1024000 | tf_op jit(solution)/shard_map/all_gather | solution.py:56
  26.4 0.0 all-gather.2.cloned.1.call-update
  26.5 0.0 copy-start.10
  26.5 0.0 reduce-scatter.4.cloned.1.call-start
  26.5 3.3 %copy.34 = bf16[3,3200,128]{1,2,0:T(8,128)(2,1)S(1)} copy(bf16[3,3200,128]{2,1,0:T(8,128)(2,1)} %param.16) | data formatting | bytes 4915200 | tf_op args[3]
  29.8 41.9 %all-gather.2.cloned.1.call-done = bf16[1,512,3200]{2,1,0:T(8,128)(2,1)} async-done(((bf16[1,128,3200]{2,1,0:T(8,128)(2,1)}), bf16[1,512,3200]{2,1,0:T(8,128)(2,1)}) %all-gather.2.cloned.1.call-update) | async-done | bytes 3276816 | tf_op jit(solution)/shard_map/all_gather | solution.py:57
  71.8 2.8 %fusion = f32[512]{0:T(512)S(1)} fusion(bf16[1,512,3200]{2,1,0:T(8,128)(2,1)} %all-gather.2.cloned.1.call-done), kind=kLoop, calls=%fused_computation.2 | loop fusion | flops 4914688 | bytes 3278848 | tf_op jit(solution)/shard_map/reduce_sum | solution.py:110
  74.6 0.1 copy-done.1
  74.7 1.7 fusion.4
  76.4 0.9 copy-done.2
  77.3 0.1 multiply_reduce_fusion.2
  77.3 9.0 %psum.14 = f32[2,512]{1,0:T(2,128)S(1)} all-reduce(f32[2,512]{1,0:T(2,128)S(1)} %pad_maximum_fusion.1), channel_id=1, replica_groups=mesh['req'=16,'ty'=4,'tz'=4] {'tz'}, use_global_device_ids=true, to_apply=%region_5.6 | all-reduce | flops 1024 | bytes 8192 | tf_op jit(solution)/shard_map/psum | solution.py:118
  86.3 8.7 %psum.15 = f32[2,512]{1,0:T(2,128)S(1)} all-reduce(f32[2,512]{1,0:T(2,128)S(1)} %psum.14), channel_id=1, replica_groups=mesh['req'=16,'ty'=4,'tz'=4] {'ty'}, use_global_device_ids=true, to_apply=%region_6.7 | all-reduce | flops 1024 | bytes 8192 | tf_op jit(solution)/shard_map/psum | solution.py:117
  95.0 1.5 fusion.118
  96.5 0.2 fusion.10
  96.7 4.0 %convolution_convert_fusion = bf16[512,3200]{0,1:T(8,128)(2,1)} fusion(bf16[128,3200]{1,0:T(8,128)(2,1)S(1)} %copy-done, f32[512,512]{0,1:T(8,128)S(1)} %get-tuple-element.35, f32[512]{0:T(512)S(1)} %fusion.10, f32[512]{0:T(512)S(1)} %get-tuple-element.34, f32[3,512,128]{1,2,0:T(8,128)} %bitcast.73), kind=kOutput, calls=%fused_computation.5 | convolution fusion | flops 489029632 | bytes 5279744 | tf_op jit(solution)/shard_map/dot_general | solution.py:150
  100.7 0.0 reduce-scatter.4.cloned.1.call-update
  100.7 41.6 %reduce-scatter.4.cloned.1.call-done = bf16[512,800]{0,1:T(8,128)(2,1)} async-done(((bf16[512,3200]{0,1:T(8,128)(2,1)}), bf16[512,800]{0,1:T(8,128)(2,1)}) %reduce-scatter.4.cloned.1.call-update) | async-done | bytes 819216 | tf_op jit(solution)/shard_map/reduce_scatter | solution.py:151
  142.4 5.4 %all-to-all-start = ((bf16[512,4,200]{0,2,1:T(8,128)(2,1)}), bf16[512,4,200]{0,2,1:T(8,128)(2,1)S(1)}, u32[]{:S(2)}, u32[]{:S(2)}) async-start(bf16[512,4,200]{0,2,1:T(8,128)(2,1)} %bitcast.68), calls=%async_computation.1 | async-start | bytes 1638400 | tf_op jit(solution)/shard_map/all_to_all | solution.py:69
  147.8 1.1 dynamic-slice_convert_fusion
  148.9 0.3 reshape.232
  149.2 0.0 copy-start.3
  149.2 0.0 copy-start.4
  149.3 16.0 %all-to-all-done = bf16[512,4,200]{0,2,1:T(8,128)(2,1)S(1)} async-done(((bf16[512,4,200]{0,2,1:T(8,128)(2,1)}), bf16[512,4,200]{0,2,1:T(8,128)(2,1)S(1)}, u32[]{:S(2)}, u32[]{:S(2)}) %all-to-all-start) | async-done | bytes 819232 | tf_op jit(solution)/shard_map/all_to_all | solution.py:69
  165.3 0.1 convert_reduce_fusion
  165.4 0.2 copy.35
  165.6 0.3 reduce_sum.108
  165.9 0.6 fusion.117
  166.5 0.1 stack.21
  166.6 0.6 multiply_reduce_fusion
  167.2 0.1 stack.22
  167.3 3.4 %collective-permute-start = (f32[1,2,128]{2,1,0:T(2,128)S(1)}, f32[1,2,128]{2,1,0:T(2,128)S(1)}, u32[]{:S(2)}, u32[]{:S(2)}) collective-permute-start(f32[1,2,128]{2,1,0:T(2,128)S(1)} %maximum_bitcast_fusion), channel_id=1, source_target_pairs={{0,1},{1,0},{2,3},{3,2},{4,5},{5,4},{6,7},{7,6},{8,9},{9,8},{10,11... | collective-permute-start | bytes 3080 | tf_op jit(solution)/shard_map/ppermute | solution.py:80
  170.7 0.1 copy.36
  170.8 1.5 collective-permute-done
  172.2 2.0 collective-permute-start.1
  174.3 2.5 collective-permute-done.1
  176.7 0.2 collective-permute-start.2
  177.0 3.4 %collective-permute-done.2 = f32[4,2,128]{2,1,0:T(2,128)S(1)} collective-permute-done((f32[4,2,128]{2,1,0:T(2,128)S(1)}, f32[4,2,128]{2,1,0:T(2,128)S(1)}, u32[]{:S(2)}, u32[]{:S(2)}) %collective-permute-start.2) | collective-permute-done | bytes 4128 | tf_op jit(solution)/shard_map/ppermute | solution.py:80
  180.3 1.4 collective-permute-start.3
  181.8 3.7 %collective-permute-done.3 = f32[8,2,128]{2,1,0:T(2,128)S(1)} collective-permute-done((f32[8,2,128]{2,1,0:T(2,128)S(1)}, f32[8,2,128]{2,1,0:T(2,128)S(1)}, u32[]{:S(2)}, u32[]{:S(2)}) %collective-permute-start.3) | collective-permute-done | bytes 8224 | tf_op jit(solution)/shard_map/ppermute | solution.py:80
  185.6 0.0 copy-start.5
  185.6 0.0 copy-start.11
  185.6 4.4 %fusion.3 = bf16[128,3072]{1,0:T(8,128)(2,1)} fusion(bf16[4,200,3072]{2,1,0:T(8,128)(2,1)} %param.23, f32[128,4,200]{2,0,1:T(8,128)S(1)} %bitcast.67, f32[4,200]{1,0:T(4,128)S(1)} %copy-done.3, f32[4,200]{1,0:T(4,128)S(1)} %copy-done.4, f32[128]{0:T(128)S(1)} %add_rsqrt_fusion.1, f32[128]{0:T(128)S(1)} %broadcast_multiply_fusion.1), kind=kOutput, calls=%fused_computation.7 | convolution fusion | flops 630050816 | bytes 6118656 | tf_op jit(solution)/shard_map/dot_general | solution.py:178
  190.0 0.0 reduce-scatter.6.cloned.1.call-update
  190.0 0.0 reduce-scatter.8.cloned.1.call-start
  190.1 0.5 broadcast.188
  190.6 0.7 reduce.15
  191.3 0.1 reshape_reshape_squeeze.3
  191.4 0.2 copy.38
  191.6 0.1 reshape.230
  191.7 0.0 copy-done.5
  191.7 0.3 dynamic-slice_reduce_fusion
  192.0 0.1 fusion.79
  192.1 0.1 fusion.86
  192.2 0.2 select_reduce_fusion
  192.3 23.3 %reduce-scatter.6.cloned.1.call-done = bf16[32,3072]{1,0:T(8,128)(2,1)} async-done(((bf16[128,3072]{1,0:T(8,128)(2,1)}), bf16[32,3072]{1,0:T(8,128)(2,1)}) %reduce-scatter.6.cloned.1.call-update) | async-done | bytes 196624 | tf_op jit(solution)/shard_map/reduce_scatter | solution.py:61
  215.7 0.0 reduce-scatter.8.cloned.1.call-update
  215.7 0.1 iota_compare_fusion.1
  215.8 24.0 %reduce-scatter.8.cloned.1.call-done = bf16[8,3072]{1,0:T(8,128)(2,1)} async-done(((bf16[32,3072]{1,0:T(8,128)(2,1)}), bf16[8,3072]{1,0:T(8,128)(2,1)}) %reduce-scatter.8.cloned.1.call-update) | async-done | bytes 49168 | tf_op jit(solution)/shard_map/reduce_scatter | solution.py:62
  239.8 1.2 convolution_convert_fusion.1
  241.0 0.2 copy.39
  241.2 22.4 %all_to_all.10 = bf16[16,2,3072]{2,1,0:T(2,128)(2,1)S(1)} all-to-all(bf16[16,2,3072]{2,1,0:T(2,128)(2,1)S(1)} %copy.39), channel_id=1, replica_groups=mesh['req'=16,'ty'=4,'tz'=4] {'req'}, dimensions={0} | all-to-all | bytes 393216 | tf_op jit(solution)/shard_map/all_to_all | solution.py:198
  263.7 0.7 copy.47
  (38 shorter events, 0.3 us)
Async XLA Ops:
  6.5 90.2 %copy-start = (bf16[128,3200]{1,0:T(8,128)(2,1)S(1)}, bf16[128,3200]{1,0:T(8,128)(2,1)}, u32[]{:S(2)}) copy-start(bf16[128,3200]{1,0:T(8,128)(2,1)} %param.18) | copy-start | bytes 2457604
  6.5 23.3 %copy-start.9 = (f32[2,128]{1,0:T(2,128)S(1)}, f32[2,128]{1,0:T(2,128)}, u32[]{:S(2)}) copy-start(f32[2,128]{1,0:T(2,128)} %param.17) | copy-start | bytes 3076
  6.5 65.2 %all-gather.2.cloned.1.call-start = ((), (), s32[]{:S(2)}) async-start(), calls=%async_computation.5 | async-start | bytes 4096000 | tf_op jit(solution)/shard_map/all_gather | solution.py:57
  26.5 48.1 %copy-start.10 = (f32[3200]{0:T(1024)S(1)}, f32[3200]{0:T(1024)}, u32[]{:S(2)}) copy-start(f32[3200]{0:T(1024)} %param.15) | copy-start | bytes 38404
  26.5 115.9 %reduce-scatter.4.cloned.1.call-start = ((), (), s32[]{:S(2)}) async-start(), calls=%async_computation.6 | async-start | bytes 4096000 | tf_op jit(solution)/shard_map/reduce_scatter | solution.py:151
  71.7 2.9 %copy-start.1 = (bf16[1,512,3200]{2,1,0:T(8,128)(2,1)S(1)}, bf16[1,512,3200]{2,1,0:T(8,128)(2,1)}, u32[]{:S(2)}) copy-start(bf16[1,512,3200]{2,1,0:T(8,128)(2,1)} %all-gather.2.cloned.1.call-done) | copy-start | bytes 9830404
  74.7 20.4 %copy-start.6 = (s32[1,512]{1,0:T(1,128)S(1)}, s32[1,512]{1,0:T(1,128)}, u32[]{:S(2)}) copy-start(s32[1,512]{1,0:T(1,128)} %param.14) | copy-start | bytes 6148
  76.3 0.9 copy-start.2
  142.4 23.5 %copy-start.7 = (f32[200]{0:T(256)S(1)}, f32[200]{0:T(256)}, u32[]{:S(2)}) copy-start(f32[200]{0:T(256)} %param.19) | copy-start | bytes 2404
  142.4 23.5 %copy-start.8 = (f32[200]{0:T(256)S(1)}, f32[200]{0:T(256)}, u32[]{:S(2)}) copy-start(f32[200]{0:T(256)} %param.20) | copy-start | bytes 2404
  142.4 22.9 %all-to-all-start = ((bf16[512,4,200]{0,2,1:T(8,128)(2,1)}), bf16[512,4,200]{0,2,1:T(8,128)(2,1)S(1)}, u32[]{:S(2)}, u32[]{:S(2)}) async-start(bf16[512,4,200]{0,2,1:T(8,128)(2,1)} %bitcast.68), calls=%async_computation.1 | async-start | bytes 1638400 | tf_op jit(solution)/shard_map/all_to_all | solution.py:69
  147.8 67.9 %reduce-scatter.6.cloned.1.call-start = ((), (), s32[]{:S(2)}) async-start(), calls=%async_computation.7 | async-start | bytes 983040 | tf_op jit(solution)/shard_map/reduce_scatter | solution.py:61
  149.2 36.4 %copy-start.3 = (f32[4,200]{1,0:T(4,128)S(1)}, f32[4,200]{1,0:T(4,128)}, u32[]{:S(2)}) copy-start(f32[4,200]{1,0:T(4,128)} %param.22) | copy-start | bytes 9604
  149.2 36.4 %copy-start.4 = (f32[4,200]{1,0:T(4,128)S(1)}, f32[4,200]{1,0:T(4,128)}, u32[]{:S(2)}) copy-start(f32[4,200]{1,0:T(4,128)} %param.21) | copy-start | bytes 9604
  167.3 4.9 %collective-permute-start = (f32[1,2,128]{2,1,0:T(2,128)S(1)}, f32[1,2,128]{2,1,0:T(2,128)S(1)}, u32[]{:S(2)}, u32[]{:S(2)}) collective-permute-start(f32[1,2,128]{2,1,0:T(2,128)S(1)} %maximum_bitcast_fusion), channel_id=1, source_target_pairs={{0,1},{1,0},{2,3},{3,2},{4,5},{5,4},{6,7},{7,6},{8,9},{9,8},{10,11... | collective-permute-start | bytes 3080 | tf_op jit(solution)/shard_map/ppermute | solution.py:80
  172.2 4.5 %collective-permute-start.1 = (f32[2,2,128]{2,1,0:T(2,128)S(1)}, f32[2,2,128]{2,1,0:T(2,128)S(1)}, u32[]{:S(2)}, u32[]{:S(2)}) collective-permute-start(f32[2,2,128]{2,1,0:T(2,128)S(1)} %pad_maximum_fusion.3), channel_id=1, source_target_pairs={{0,2},{1,3},{2,0},{3,1},{4,6},{5,7},{6,4},{7,5},{8,10},{9,11},{10,... | collective-permute-start | bytes 6152 | tf_op jit(solution)/shard_map/ppermute | solution.py:80
  176.7 3.6 %collective-permute-start.2 = (f32[4,2,128]{2,1,0:T(2,128)S(1)}, f32[4,2,128]{2,1,0:T(2,128)S(1)}, u32[]{:S(2)}, u32[]{:S(2)}) collective-permute-start(f32[4,2,128]{2,1,0:T(2,128)S(1)} %pad_maximum_fusion.2), channel_id=1, source_target_pairs={{0,4},{4,0},{8,12},{12,8},{1,5},{5,1},{9,13},{13,9},{2,6},{6,2},{1... | collective-permute-start | bytes 12296 | tf_op jit(solution)/shard_map/ppermute | solution.py:80
  180.3 5.2 %collective-permute-start.3 = (f32[8,2,128]{2,1,0:T(2,128)S(1)}, f32[8,2,128]{2,1,0:T(2,128)S(1)}, u32[]{:S(2)}, u32[]{:S(2)}) collective-permute-start(f32[8,2,128]{2,1,0:T(2,128)S(1)} %pad_maximum_fusion), channel_id=1, source_target_pairs={{0,8},{4,12},{8,0},{12,4},{1,9},{5,13},{9,1},{13,5},{2,10},{6,14},... | collective-permute-start | bytes 24584 | tf_op jit(solution)/shard_map/ppermute | solution.py:80
  185.6 6.1 %copy-start.5 = (s32[16,8,1]{0,2,1:T(1,128)S(1)}, s32[16,8,1]{0,2,1:T(1,128)}, u32[]{:S(2)}) copy-start(s32[16,8,1]{0,2,1:T(1,128)} %param.25) | copy-start | bytes 1540
  185.6 54.2 %copy-start.11 = (f32[3072]{0:T(1024)S(1)}, f32[3072]{0:T(1024)}, u32[]{:S(2)}) copy-start(f32[3072]{0:T(1024)} %param.24) | copy-start | bytes 36868
  190.0 49.7 %reduce-scatter.8.cloned.1.call-start = ((), (), s32[]{:S(2)}) async-start(), calls=%async_computation.8 | async-start | bytes 245760 | tf_op jit(solution)/shard_map/reduce_scatter | solution.py:62
Sparse Core Ops, SparseCore 0:
  26.6 45.1 all-gather.1
  100.9 41.4 reduce-scatter.3
  190.2 25.4 reduce-scatter.5
  218.0 21.7 reduce-scatter.7

commit v3 on v2

--- a/solution.py
+++ b/solution.py
@@ -52,9 +52,35 @@
     return jnp.sum(before * owner_hits, axis=1)
 
 
+def axis_exchange(value, axis_name):
+    count = lax.axis_size(axis_name)
+    got = [value]
+    for shift in range(1, count):
+        ring = [(i, (i + shift) % count) for i in range(count)]
+        got.append(lax.ppermute(value, axis_name, ring))
+    return got
+
+
 def tp_gather(value, axis):
-    inner = lax.all_gather(value, "tz", axis=axis, tiled=True)
+    count = lax.axis_size("tz")
+    got = axis_exchange(value, "tz")
+    ordered = jnp.stack([got[(count - k) % count] for k in range(count)], axis=0)
+    ordered = jnp.roll(ordered, lax.axis_index("tz"), axis=0)
+    inner = jnp.concatenate([ordered[k] for k in range(count)], axis=axis)
     return lax.all_gather(inner, "ty", axis=axis, tiled=True)
+
+
+def exchange_sum(value):
+    for axis_name in ("tz", "ty"):
+        got = axis_exchange(value, axis_name)
+        value = sum(got[1:], got[0])
+    return value
+
+
+def exchange_gather(value):
+    for axis_name in ("tz", "ty"):
+        value = jnp.concatenate(axis_exchange(value, axis_name), axis=0)
+    return value
 
 
 def tp_scatter_sum(value, axis):
@@ -114,9 +140,8 @@
     q_part = proj_qkv[0]
     k_part = proj_qkv[1]
     v_part = proj_qkv[2]
-    square_sums = lax.psum(
-        lax.psum(jnp.stack([jnp.sum(q_part * q_part, axis=-1), jnp.sum(k_part * k_part, axis=-1)]), "tz"),
-        "ty",
+    square_sums = exchange_sum(
+        jnp.stack([jnp.sum(q_part * q_part, axis=-1), jnp.sum(k_part * k_part, axis=-1)])
     )
     inner_width = HEADS * HD
     q_scaled = (
@@ -161,7 +186,7 @@
     local_mean = local_sum / local_count
     local_dev = merged - local_mean[:, None, None]
     local_m2 = jnp.sum(local_dev * local_dev, axis=(1, 2))
-    stats = butterfly_gather(jnp.stack([local_sum, local_m2])[None])
+    stats = exchange_gather(jnp.stack([local_sum, local_m2])[None])
     row_mean = jnp.sum(stats[:, 0], axis=0) / feature_total
     spread = stats[:, 0] / local_count - row_mean[None, :]
     row_m2 = jnp.sum(stats[:, 1], axis=0) + local_count * jnp.sum(spread * spread, axis=0)
@@ -174,10 +199,9 @@
     flat_rows = normal_rows.reshape(merged_total, 4 * width_dev)
     flat_weight = w_merge.reshape(4 * width_dev, w_merge.shape[2])
     merged_dev = merged_total // tp_total
-    own_rows = tp_scatter_sum(
-        jnp.dot(flat_rows, flat_weight, preferred_element_type=jnp.float32).astype(jnp.bfloat16),
-        0,
-    ).astype(jnp.float32)
+    row_part = jnp.dot(flat_rows, flat_weight, preferred_element_type=jnp.float32)
+    row_outer = lax.psum_scatter(row_part.astype(jnp.bfloat16), "ty", scatter_dimension=0, tiled=True)
+    own_rows = scatter_sum_exchange(row_outer, "tz", 0)
     first_tokens = merge_rows(group_segs.reshape(seq_len, 1))[:, 0, 0]
     own_first = lax.dynamic_slice_in_dim(first_tokens, tp_index * merged_dev, merged_dev, 0)
     live_rows = (own_first >= 0).astype(jnp.float32)

time: 271 us -> 252 us (0.930)
  blocking collectives: 60 us -> 21.2 us
  starting transfers between devices: 12.5 us -> 35.6 us
  waiting for transfers between devices: 158 us -> 153 us
    reduce_scatter x2 -> x1, waiting for transfers between devices: 47.3 us -> 23.5 us  [per_device(): lax.psum_scatter(row_part.astype(jnp.bfloat16), 'ty', scatter_dimension=0...]
    all_gather x1 -> x0, blocking collectives: 19.9 us -> none  [tp_gather(): inner = lax.all_gather(value, 'tz', axis=axis, tiled=True)]
    ppermute x4 -> x15, starting transfers between devices: 7.06 us -> 25 us  [axis_exchange(): got.append(lax.ppermute(value, axis_name, ring))]
    psum x2 -> x0, blocking collectives: 17.7 us -> none  [the longest x1 8.98 us: per_device(): lax.psum(jnp.stack([jnp.sum(q_part * q_part, axis=-1), jnp.sum(k_part * k...]
    ppermute x4 -> x15, waiting for transfers between devices: 11 us -> 24.8 us  [axis_exchange(): got.append(lax.ppermute(value, axis_name, ring))]
    all_to_all x1 -> x2, waiting for transfers between devices: 16 us -> 21.5 us  [scatter_sum_exchange(): lax.all_to_all(parts, axis_name, split_axis=axis, concat_axis=axis, tiled...]
    all_to_all x1 -> x2, starting transfers between devices: 5.39 us -> 10.6 us  [scatter_sum_exchange(): lax.all_to_all(parts, axis_name, split_axis=axis, concat_axis=axis, tiled...]
    unnamed x30 -> x41, local copies, waits for them, and re-layouts: 5.55 us -> 6.51 us
  transfers between devices with their start and end apart: 9 -> 20, of which waited for: 9 -> 17; matrix products, arithmetic and copies ran while one was open for 3% -> 3% of each run, Pallas kernels for 0% -> 0%
where the time goes in v3:
time: 252 us; the launch traced here: 251 us
  waiting for transfers between devices  153 us (61%)
  starting transfers between devices  35.6 us (14%)
  blocking collectives  21.2 us (8%)
  between operations  13.4 us (5%)
  matrix products  11.7 us (5%)
  local copies, waits for them, and re-layouts  8.54 us (3%)
  other arithmetic  7.74 us (3%)
    reduce_scatter x1, waiting for transfers between devices, per_device(): lax.psum_scatter(head_part.astype(jnp.bfloat16), 'ty', scatter_dimension=...  41.8 us
    all_gather x1, waiting for transfers between devices, tp_gather(): return lax.all_gather(inner, 'ty', axis=axis, tiled=True)  41.3 us
    ppermute x15, starting transfers between devices, axis_exchange(): got.append(lax.ppermute(value, axis_name, ring))  25 us
    ppermute x15, waiting for transfers between devices, axis_exchange(): got.append(lax.ppermute(value, axis_name, ring))  24.8 us
    reduce_scatter x1, waiting for transfers between devices, per_device(): lax.psum_scatter(row_part.astype(jnp.bfloat16), 'ty', scatter_dimension=0...  23.5 us
    all_to_all x2, waiting for transfers between devices, scatter_sum_exchange(): lax.all_to_all(parts, axis_name, split_axis=axis, concat_axis=axis, tiled...  21.5 us
    all_to_all x1, blocking collectives, per_device(): lax.all_to_all(outgoing, 'req', split_axis=0, concat_axis=0, tiled=True)  21.2 us
    all_to_all x2, starting transfers between devices, scatter_sum_exchange(): lax.all_to_all(parts, axis_name, split_axis=axis, concat_axis=axis, tiled...  10.6 us
  transfers between devices with their start and end apart: 20, of which 17 were waited for; matrix products, arithmetic and copies ran while one was open for 3% of the time, Pallas kernels for 0%

profile of v3, /device:TPU:32, one launch (start us, length us, event | category | flops | bytes accessed | tf_op | source)
XLA Modules:
  0.0 251.1 jit_solution(8925830277426510005)
XLA Ops:
  6.5 1.8 collective-permute-start
  8.4 1.6 collective-permute-start.1
  9.9 2.8 %collective-permute-start.2 = (bf16[1,32,3200]{2,1,0:T(8,128)(2,1)}, bf16[1,32,3200]{2,1,0:T(8,128)(2,1)S(1)}, u32[]{:S(2)}, u32[]{:S(2)}) collective-permute-start(bf16[1,32,3200]{2,1,0:T(8,128)(2,1)} %param.13), channel_id=1, source_target_pairs={{0,1},{1,2},{2,3},{3,0},{4,5},{5,6},{6,7},{7,4},{8,9},{9,10},{10,1... | collective-permute-start | bytes 614408 | tf_op jit(solution)/shard_map/ppermute | solution.py:60
  12.7 1.0 bitcast_dynamic-update-slice_fusion.6
  13.7 1.0 collective-permute-done
  14.8 9.5 %collective-permute-done.1 = bf16[1,32,3200]{2,1,0:T(8,128)(2,1)S(1)} collective-permute-done((bf16[1,32,3200]{2,1,0:T(8,128)(2,1)}, bf16[1,32,3200]{2,1,0:T(8,128)(2,1)S(1)}, u32[]{:S(2)}, u32[]{:S(2)}) %collective-permute-start.1) | collective-permute-done | bytes 204832 | tf_op jit(solution)/shard_map/ppermute | solution.py:60
  24.3 3.5 %collective-permute-done.2 = bf16[1,32,3200]{2,1,0:T(8,128)(2,1)S(1)} collective-permute-done((bf16[1,32,3200]{2,1,0:T(8,128)(2,1)}, bf16[1,32,3200]{2,1,0:T(8,128)(2,1)S(1)}, u32[]{:S(2)}, u32[]{:S(2)}) %collective-permute-start.2) | collective-permute-done | bytes 204832 | tf_op jit(solution)/shard_map/ppermute | solution.py:60
  28.0 1.0 pad_maximum_fusion
  29.0 1.0 copy-done.2
  30.0 3.1 %copy.34 = bf16[3,3200,128]{1,2,0:T(8,128)(2,1)} copy(bf16[3,3200,128]{2,1,0:T(8,128)(2,1)S(1)} %copy-done.2) | data formatting | bytes 4915200 | tf_op args[3]
  33.0 41.3 %all-gather.2.cloned.1.call-done = bf16[1,512,3200]{2,1,0:T(8,128)(2,1)} async-done(((bf16[1,128,3200]{2,1,0:T(8,128)(2,1)}), bf16[1,512,3200]{2,1,0:T(8,128)(2,1)}) %all-gather.2.cloned.1.call-update) | async-done | bytes 3276816 | tf_op jit(solution)/shard_map/all_gather | solution.py:70
  74.4 2.8 %fusion = f32[512]{0:T(512)S(1)} fusion(bf16[1,512,3200]{2,1,0:T(8,128)(2,1)} %all-gather.2.cloned.1.call-done), kind=kLoop, calls=%fused_computation.2 | loop fusion | flops 4914688 | bytes 3278848 | tf_op jit(solution)/shard_map/reduce_sum | solution.py:136
  77.2 0.1 copy-done.1
  77.3 3.4 %fusion.4 = f32[512,384]{0,1:S(1)} fusion(bf16[3200,384]{0,1:T(8,128)(2,1)} %bitcast.87, bf16[1,512,3200]{2,1,0:T(8,128)(2,1)S(1)} %copy-done.1, f32[3200]{0:T(1024)S(1)} %copy-done.11, f32[512]{0:T(512)S(1)} %add_rsqrt_fusion), kind=kOutput, calls=%fused_computation.9 | convolution fusion | flops 1264844800 | bytes 6535680
  80.8 0.5 collective-permute-start.5
  81.3 2.5 %collective-permute-start.4 = (f32[2,512]{1,0:T(2,128)S(1)}, f32[2,512]{1,0:T(2,128)S(1)}, u32[]{:S(2)}, u32[]{:S(2)}) collective-permute-start(f32[2,512]{1,0:T(2,128)S(1)} %pad_maximum_fusion.1), channel_id=1, source_target_pairs={{0,2},{1,3},{2,0},{3,1},{4,6},{5,7},{6,4},{7,5},{8,10},{9,11},{10,... | collective-permute-start | bytes 12296 | tf_op jit(solution)/shard_map/ppermute | solution.py:60
  83.8 2.5 collective-permute-start.3
  86.3 1.3 collective-permute-done.3
  87.6 1.0 collective-permute-start.8
  88.7 1.8 collective-permute-start.7
  90.5 0.6 collective-permute-start.6
  91.1 0.3 collective-permute-done.8
  91.3 2.5 collective-permute-done.7
  93.8 1.5 collective-permute-done.6
  95.3 0.4 fusion.114
  95.8 0.2 fusion.10
  96.0 3.1 %convolution_convert_fusion = bf16[512,3200]{0,1:T(8,128)(2,1)} fusion(bf16[128,3200]{1,0:T(8,128)(2,1)S(1)} %copy-done, f32[512,512]{0,1:T(8,128)S(1)} %get-tuple-element.39, f32[512]{0:T(512)S(1)} %fusion.10, f32[512]{0:T(512)S(1)} %get-tuple-element.38, f32[3,512,128]{1,2,0:T(8,128)S(1)} %bitcast.94), kind=kOutput, calls=%fused_computation.5 | convolution fusion | flops 489029632 | bytes 5279744 | tf_op jit(solution)/shard_map/dot_general | solution.py:175
  99.1 41.8 %reduce-scatter.3.cloned.1.call-done = bf16[512,800]{0,1:T(8,128)(2,1)} async-done(((bf16[512,3200]{0,1:T(8,128)(2,1)}), bf16[512,800]{0,1:T(8,128)(2,1)}) %reduce-scatter.3.cloned.1.call-update) | async-done | bytes 819216 | tf_op jit(solution)/shard_map/reduce_scatter | solution.py:176
  140.9 5.3 %all-to-all-start = ((bf16[512,4,200]{0,2,1:T(8,128)(2,1)}), bf16[512,4,200]{0,2,1:T(8,128)(2,1)S(1)}, u32[]{:S(2)}, u32[]{:S(2)}) async-start(bf16[512,4,200]{0,2,1:T(8,128)(2,1)} %bitcast.89), calls=%async_computation.1 | async-start | bytes 1638400 | tf_op jit(solution)/shard_map/all_to_all | solution.py:95
  146.1 1.1 dynamic-slice_convert_fusion
  147.3 0.3 reshape.236
  147.6 16.0 %all-to-all-done = bf16[512,4,200]{0,2,1:T(8,128)(2,1)S(1)} async-done(((bf16[512,4,200]{0,2,1:T(8,128)(2,1)}), bf16[512,4,200]{0,2,1:T(8,128)(2,1)S(1)}, u32[]{:S(2)}, u32[]{:S(2)}) %all-to-all-start) | async-done | bytes 819232 | tf_op jit(solution)/shard_map/all_to_all | solution.py:95
  163.6 0.1 convert_reduce_fusion
  163.7 0.2 copy.35
  163.9 0.3 reduce_sum.117
  164.3 0.6 fusion.113
  164.9 0.1 stack.38
  165.0 0.6 multiply_reduce_fusion
  165.6 0.1 stack.39
  165.7 1.5 collective-permute-start.9
  167.2 4.2 %collective-permute-start.10 = (f32[1,2,128]{2,1,0:T(2,128)S(1)}, f32[1,2,128]{2,1,0:T(2,128)S(1)}, u32[]{:S(2)}, u32[]{:S(2)}) collective-permute-start(f32[1,2,128]{2,1,0:T(2,128)S(1)} %maximum_bitcast_fusion), channel_id=1, source_target_pairs={{0,2},{1,3},{2,0},{3,1},{4,6},{5,7},{6,4},{7,5},{8,10},{9,11},{10,... | collective-permute-start | bytes 3080 | tf_op jit(solution)/shard_map/ppermute | solution.py:60
  171.5 1.5 collective-permute-done.10
  173.0 2.0 collective-permute-done.11
  175.0 0.2 collective-permute-start.12
  175.2 2.1 collective-permute-start.13
  177.3 1.8 collective-permute-start.14
  179.1 0.7 collective-permute-done.12
  179.8 0.5 collective-permute-done.13
  180.3 0.6 collective-permute-done.14
  181.0 4.4 %fusion.3 = bf16[128,3072]{1,0:T(8,128)(2,1)} fusion(bf16[4,200,3072]{2,1,0:T(8,128)(2,1)} %param.23, f32[128,4,200]{2,0,1:T(8,128)S(1)} %bitcast.88, f32[4,200]{1,0:T(4,128)S(1)} %copy-done.4, f32[4,200]{1,0:T(4,128)S(1)} %copy-done.5, f32[128]{0:T(128)S(1)} %add_rsqrt_fusion.1, f32[128]{0:T(128)S(1)} %broadcast_multiply_fusion.1), kind=kOutput, calls=%fused_computation.7 | convolution fusion | flops 630050816 | bytes 6118656 | tf_op jit(solution)/shard_map/dot_general | solution.py:202
  185.4 0.5 broadcast.189
  185.9 0.7 reduce.15
  186.6 0.1 reshape_reshape_squeeze.3
  186.7 0.2 copy.38
  186.9 0.1 reshape.234
  187.0 0.3 dynamic-slice_reduce_fusion
  187.4 0.2 select_reduce_fusion
  187.6 23.5 %reduce-scatter.5.cloned.1.call-done = bf16[32,3072]{1,0:T(8,128)(2,1)} async-done(((bf16[128,3072]{1,0:T(8,128)(2,1)}), bf16[32,3072]{1,0:T(8,128)(2,1)}) %reduce-scatter.5.cloned.1.call-update) | async-done | bytes 196624 | tf_op jit(solution)/shard_map/reduce_scatter | solution.py:203
  211.1 5.3 %all-to-all-start.1 = ((bf16[4,8,3072]{2,1,0:T(8,128)(2,1)}), bf16[4,8,3072]{2,1,0:T(8,128)(2,1)S(1)}, u32[]{:S(2)}, u32[]{:S(2)}) async-start(bf16[4,8,3072]{2,1,0:T(8,128)(2,1)} %bitcast.95), calls=%async_computation.3 | async-start | bytes 393216 | tf_op jit(solution)/shard_map/all_to_all | solution.py:95
  216.5 5.5 %all-to-all-done.1 = bf16[4,8,3072]{2,1,0:T(8,128)(2,1)S(1)} async-done(((bf16[4,8,3072]{2,1,0:T(8,128)(2,1)}), bf16[4,8,3072]{2,1,0:T(8,128)(2,1)S(1)}, u32[]{:S(2)}, u32[]{:S(2)}) %all-to-all-start.1) | async-done | bytes 196640 | tf_op jit(solution)/shard_map/all_to_all | solution.py:95
  222.1 0.4 convolution_convert_fusion.1
  222.6 0.2 copy.39
  222.8 21.2 %all_to_all.15 = bf16[16,2,3072]{2,1,0:T(2,128)(2,1)S(1)} all-to-all(bf16[16,2,3072]{2,1,0:T(2,128)(2,1)S(1)} %copy.39), channel_id=1, replica_groups=mesh['req'=16,'ty'=4,'tz'=4] {'req'}, dimensions={0} | all-to-all | bytes 393216 | tf_op jit(solution)/shard_map/all_to_all | solution.py:222
  243.9 0.7 copy.56
  (71 shorter events, 1.0 us)
Async XLA Ops:
  6.5 89.4 %copy-start = (bf16[128,3200]{1,0:T(8,128)(2,1)S(1)}, bf16[128,3200]{1,0:T(8,128)(2,1)}, u32[]{:S(2)}) copy-start(bf16[128,3200]{1,0:T(8,128)(2,1)} %param.18) | copy-start | bytes 2457604
  6.5 21.3 %copy-start.3 = (bf16[1,32,3200]{2,1,0:T(8,128)(2,1)S(1)}, bf16[1,32,3200]{2,1,0:T(8,128)(2,1)}, u32[]{:S(2)}) copy-start(bf16[1,32,3200]{2,1,0:T(8,128)(2,1)} %param.13) | copy-start | bytes 614404
  6.5 67.8 %all-gather.2.cloned.1.call-start = ((), (), s32[]{:S(2)}) async-start(), calls=%async_computation.5 | async-start | bytes 4096000 | tf_op jit(solution)/shard_map/all_gather | solution.py:70
  6.5 8.2 %collective-permute-start = (bf16[1,32,3200]{2,1,0:T(8,128)(2,1)}, bf16[1,32,3200]{2,1,0:T(8,128)(2,1)S(1)}, u32[]{:S(2)}, u32[]{:S(2)}) collective-permute-start(bf16[1,32,3200]{2,1,0:T(8,128)(2,1)} %param.13), channel_id=1, source_target_pairs={{0,3},{1,0},{2,1},{3,2},{4,7},{5,4},{6,5},{7,6},{8,11},{9,8},{10,9... | collective-permute-start | bytes 614408 | tf_op jit(solution)/shard_map/ppermute | solution.py:60
  8.4 15.9 %collective-permute-start.1 = (bf16[1,32,3200]{2,1,0:T(8,128)(2,1)}, bf16[1,32,3200]{2,1,0:T(8,128)(2,1)S(1)}, u32[]{:S(2)}, u32[]{:S(2)}) collective-permute-start(bf16[1,32,3200]{2,1,0:T(8,128)(2,1)} %param.13), channel_id=1, source_target_pairs={{0,2},{1,3},{2,0},{3,1},{4,6},{5,7},{6,4},{7,5},{8,10},{9,11},{10,... | collective-permute-start | bytes 614408 | tf_op jit(solution)/shard_map/ppermute | solution.py:60
  9.9 17.8 %collective-permute-start.2 = (bf16[1,32,3200]{2,1,0:T(8,128)(2,1)}, bf16[1,32,3200]{2,1,0:T(8,128)(2,1)S(1)}, u32[]{:S(2)}, u32[]{:S(2)}) collective-permute-start(bf16[1,32,3200]{2,1,0:T(8,128)(2,1)} %param.13), channel_id=1, source_target_pairs={{0,1},{1,2},{2,3},{3,0},{4,5},{5,6},{6,7},{7,4},{8,9},{9,10},{10,1... | collective-permute-start | bytes 614408 | tf_op jit(solution)/shard_map/ppermute | solution.py:60
  28.0 2.0 copy-start.2
  29.0 111.9 %reduce-scatter.3.cloned.1.call-start = ((), (), s32[]{:S(2)}) async-start(), calls=%async_computation.6 | async-start | bytes 4096000 | tf_op jit(solution)/shard_map/reduce_scatter | solution.py:176
  30.0 47.2 %copy-start.11 = (f32[3200]{0:T(1024)S(1)}, f32[3200]{0:T(1024)}, u32[]{:S(2)}) copy-start(f32[3200]{0:T(1024)} %param.15) | copy-start | bytes 38404
  74.4 2.9 %copy-start.1 = (bf16[1,512,3200]{2,1,0:T(8,128)(2,1)S(1)}, bf16[1,512,3200]{2,1,0:T(8,128)(2,1)}, u32[]{:S(2)}) copy-start(bf16[1,512,3200]{2,1,0:T(8,128)(2,1)} %all-gather.2.cloned.1.call-done) | copy-start | bytes 9830404
  77.3 13.8 %copy-start.10 = (f32[2,128]{1,0:T(2,128)S(1)}, f32[2,128]{1,0:T(2,128)}, u32[]{:S(2)}) copy-start(f32[2,128]{1,0:T(2,128)} %param.17) | copy-start | bytes 3076
  77.3 18.1 %copy-start.7 = (s32[1,512]{1,0:T(1,128)S(1)}, s32[1,512]{1,0:T(1,128)}, u32[]{:S(2)}) copy-start(s32[1,512]{1,0:T(1,128)} %param.14) | copy-start | bytes 6148
  80.8 5.6 %collective-permute-start.5 = (f32[2,512]{1,0:T(2,128)S(1)}, f32[2,512]{1,0:T(2,128)S(1)}, u32[]{:S(2)}, u32[]{:S(2)}) collective-permute-start(f32[2,512]{1,0:T(2,128)S(1)} %pad_maximum_fusion.1), channel_id=1, source_target_pairs={{0,3},{1,0},{2,1},{3,2},{4,7},{5,4},{6,5},{7,6},{8,11},{9,8},{10,9... | collective-permute-start | bytes 12296 | tf_op jit(solution)/shard_map/ppermute | solution.py:60
  81.3 5.0 %collective-permute-start.4 = (f32[2,512]{1,0:T(2,128)S(1)}, f32[2,512]{1,0:T(2,128)S(1)}, u32[]{:S(2)}, u32[]{:S(2)}) collective-permute-start(f32[2,512]{1,0:T(2,128)S(1)} %pad_maximum_fusion.1), channel_id=1, source_target_pairs={{0,2},{1,3},{2,0},{3,1},{4,6},{5,7},{6,4},{7,5},{8,10},{9,11},{10,... | collective-permute-start | bytes 12296 | tf_op jit(solution)/shard_map/ppermute | solution.py:60
  83.8 3.8 %collective-permute-start.3 = (f32[2,512]{1,0:T(2,128)S(1)}, f32[2,512]{1,0:T(2,128)S(1)}, u32[]{:S(2)}, u32[]{:S(2)}) collective-permute-start(f32[2,512]{1,0:T(2,128)S(1)} %pad_maximum_fusion.1), channel_id=1, source_target_pairs={{0,1},{1,2},{2,3},{3,0},{4,5},{5,6},{6,7},{7,4},{8,9},{9,10},{10,1... | collective-permute-start | bytes 12296 | tf_op jit(solution)/shard_map/ppermute | solution.py:60
  87.6 3.7 %collective-permute-start.8 = (f32[2,512]{1,0:T(2,128)S(1)}, f32[2,512]{1,0:T(2,128)S(1)}, u32[]{:S(2)}, u32[]{:S(2)}) collective-permute-start(f32[2,512]{1,0:T(2,128)S(1)} %add_add_fusion.1), channel_id=1, source_target_pairs={{0,12},{4,0},{8,4},{12,8},{1,13},{5,1},{9,5},{13,9},{2,14},{6,2},{... | collective-permute-start | bytes 12296 | tf_op jit(solution)/shard_map/ppermute | solution.py:60
  88.7 5.1 %collective-permute-start.7 = (f32[2,512]{1,0:T(2,128)S(1)}, f32[2,512]{1,0:T(2,128)S(1)}, u32[]{:S(2)}, u32[]{:S(2)}) collective-permute-start(f32[2,512]{1,0:T(2,128)S(1)} %add_add_fusion.1), channel_id=1, source_target_pairs={{0,8},{4,12},{8,0},{12,4},{1,9},{5,13},{9,1},{13,5},{2,10},{6,14},... | collective-permute-start | bytes 12296 | tf_op jit(solution)/shard_map/ppermute | solution.py:60
  90.5 4.8 %collective-permute-start.6 = (f32[2,512]{1,0:T(2,128)S(1)}, f32[2,512]{1,0:T(2,128)S(1)}, u32[]{:S(2)}, u32[]{:S(2)}) collective-permute-start(f32[2,512]{1,0:T(2,128)S(1)} %add_add_fusion.1), channel_id=1, source_target_pairs={{0,4},{4,8},{8,12},{12,0},{1,5},{5,9},{9,13},{13,1},{2,6},{6,10},{... | collective-permute-start | bytes 12296 | tf_op jit(solution)/shard_map/ppermute | solution.py:60
  140.9 22.7 %all-to-all-start = ((bf16[512,4,200]{0,2,1:T(8,128)(2,1)}), bf16[512,4,200]{0,2,1:T(8,128)(2,1)S(1)}, u32[]{:S(2)}, u32[]{:S(2)}) async-start(bf16[512,4,200]{0,2,1:T(8,128)(2,1)} %bitcast.89), calls=%async_computation.1 | async-start | bytes 1638400 | tf_op jit(solution)/shard_map/all_to_all | solution.py:95
  146.1 65.0 %reduce-scatter.5.cloned.1.call-start = ((), (), s32[]{:S(2)}) async-start(), calls=%async_computation.7 | async-start | bytes 983040 | tf_op jit(solution)/shard_map/reduce_scatter | solution.py:203
  147.6 16.7 %copy-start.8 = (f32[200]{0:T(256)S(1)}, f32[200]{0:T(256)}, u32[]{:S(2)}) copy-start(f32[200]{0:T(256)} %param.19) | copy-start | bytes 2404
  147.6 16.7 %copy-start.9 = (f32[200]{0:T(256)S(1)}, f32[200]{0:T(256)}, u32[]{:S(2)}) copy-start(f32[200]{0:T(256)} %param.20) | copy-start | bytes 2404
  164.3 16.7 %copy-start.4 = (f32[4,200]{1,0:T(4,128)S(1)}, f32[4,200]{1,0:T(4,128)}, u32[]{:S(2)}) copy-start(f32[4,200]{1,0:T(4,128)} %param.22) | copy-start | bytes 9604
  164.3 16.7 %copy-start.5 = (f32[4,200]{1,0:T(4,128)S(1)}, f32[4,200]{1,0:T(4,128)}, u32[]{:S(2)}) copy-start(f32[4,200]{1,0:T(4,128)} %param.21) | copy-start | bytes 9604
  165.7 5.8 %collective-permute-start.9 = (f32[1,2,128]{2,1,0:T(2,128)S(1)}, f32[1,2,128]{2,1,0:T(2,128)S(1)}, u32[]{:S(2)}, u32[]{:S(2)}) collective-permute-start(f32[1,2,128]{2,1,0:T(2,128)S(1)} %maximum_bitcast_fusion), channel_id=1, source_target_pairs={{0,1},{1,2},{2,3},{3,0},{4,5},{5,6},{6,7},{7,4},{8,9},{9,10},{10,1... | collective-permute-start | bytes 3080 | tf_op jit(solution)/shard_map/ppermute | solution.py:60
  167.2 5.7 %collective-permute-start.10 = (f32[1,2,128]{2,1,0:T(2,128)S(1)}, f32[1,2,128]{2,1,0:T(2,128)S(1)}, u32[]{:S(2)}, u32[]{:S(2)}) collective-permute-start(f32[1,2,128]{2,1,0:T(2,128)S(1)} %maximum_bitcast_fusion), channel_id=1, source_target_pairs={{0,2},{1,3},{2,0},{3,1},{4,6},{5,7},{6,4},{7,5},{8,10},{9,11},{10,... | collective-permute-start | bytes 3080 | tf_op jit(solution)/shard_map/ppermute | solution.py:60
  171.4 3.6 %collective-permute-start.11 = (f32[1,2,128]{2,1,0:T(2,128)S(1)}, f32[1,2,128]{2,1,0:T(2,128)S(1)}, u32[]{:S(2)}, u32[]{:S(2)}) collective-permute-start(f32[1,2,128]{2,1,0:T(2,128)S(1)} %maximum_bitcast_fusion), channel_id=1, source_target_pairs={{0,3},{1,0},{2,1},{3,2},{4,7},{5,4},{6,5},{7,6},{8,11},{9,8},{10,9... | collective-permute-start | bytes 3080 | tf_op jit(solution)/shard_map/ppermute | solution.py:60
  175.0 4.8 %collective-permute-start.12 = (f32[4,2,128]{2,1,0:T(2,128)S(1)}, f32[4,2,128]{2,1,0:T(2,128)S(1)}, u32[]{:S(2)}, u32[]{:S(2)}) collective-permute-start(f32[4,2,128]{2,1,0:T(2,128)S(1)} %pad_maximum_fusion.2), channel_id=1, source_target_pairs={{0,4},{4,8},{8,12},{12,0},{1,5},{5,9},{9,13},{13,1},{2,6},{6,10},{... | collective-permute-start | bytes 12296 | tf_op jit(solution)/shard_map/ppermute | solution.py:60
  175.2 5.1 %collective-permute-start.13 = (f32[4,2,128]{2,1,0:T(2,128)S(1)}, f32[4,2,128]{2,1,0:T(2,128)S(1)}, u32[]{:S(2)}, u32[]{:S(2)}) collective-permute-start(f32[4,2,128]{2,1,0:T(2,128)S(1)} %pad_maximum_fusion.2), channel_id=1, source_target_pairs={{0,8},{4,12},{8,0},{12,4},{1,9},{5,13},{9,1},{13,5},{2,10},{6,14},... | collective-permute-start | bytes 12296 | tf_op jit(solution)/shard_map/ppermute | solution.py:60
  177.3 3.6 %collective-permute-start.14 = (f32[4,2,128]{2,1,0:T(2,128)S(1)}, f32[4,2,128]{2,1,0:T(2,128)S(1)}, u32[]{:S(2)}, u32[]{:S(2)}) collective-permute-start(f32[4,2,128]{2,1,0:T(2,128)S(1)} %pad_maximum_fusion.2), channel_id=1, source_target_pairs={{0,12},{4,0},{8,4},{12,8},{1,13},{5,1},{9,5},{13,9},{2,14},{6,2},{... | collective-permute-start | bytes 12296 | tf_op jit(solution)/shard_map/ppermute | solution.py:60
  181.0 6.0 %copy-start.6 = (s32[16,8,1]{0,2,1:T(1,128)S(1)}, s32[16,8,1]{0,2,1:T(1,128)}, u32[]{:S(2)}) copy-start(s32[16,8,1]{0,2,1:T(1,128)} %param.25) | copy-start | bytes 1540
  185.4 36.7 %copy-start.12 = (f32[3072]{0:T(1024)S(1)}, f32[3072]{0:T(1024)}, u32[]{:S(2)}) copy-start(f32[3072]{0:T(1024)} %param.24) | copy-start | bytes 36868
  211.1 11.0 %all-to-all-start.1 = ((bf16[4,8,3072]{2,1,0:T(8,128)(2,1)}), bf16[4,8,3072]{2,1,0:T(8,128)(2,1)S(1)}, u32[]{:S(2)}, u32[]{:S(2)}) async-start(bf16[4,8,3072]{2,1,0:T(8,128)(2,1)} %bitcast.95), calls=%async_computation.3 | async-start | bytes 393216 | tf_op jit(solution)/shard_map/all_to_all | solution.py:95
Sparse Core Ops, SparseCore 0:
  29.1 45.2 all-gather.1
  99.2 41.6 reduce-scatter.2
  185.5 25.4 reduce-scatter.4
